TPU v7x, 1024 devices: a whole 4x8x16 slice. The times are simulated.
1024 devices in a mesh: kloop: 256 (over z, y_hi, x), pair: 4 (over y_lo, core).
Axes of the slice: x: 4, y: 8 (y_hi: 4, y_lo: 2; y = y_hi * 2 + y_lo), z: 16, core: 2. Of those that a mesh axis runs over, the one named last changes fastest.
Arguments:
- orbitals: bfloat16 [512, 32, 512], P('kloop'), may hold values from -6 to 6
- fitting: bfloat16 [512, 1400], replicated, may hold values from -0.25 to 0.25
- screen: bfloat16 [4, 1400, 1400], P(None, None, 'pair'), may hold values from -0.00390625 to 0.00390625
- coulomb: float32 [1400], replicated, may hold values from 0.005 to 0.1
- qindex: int32 [512, 2], replicated, may hold values from 0 to 3
Outputs:
- kernel: bfloat16 [512, 2, 256, 256], P('kloop', None, 'pair')
Inputs may be any that keep to these rules, and one draw needn't show every extreme that they name: `qindex`: the index of the held screened interaction for each block.
All inputs are finite; a program needn't handle non-finite values.
Results may differ from a plain program's by a relative error of at most 0.0085.
Values may be sent and summed in bfloat16 or wider, within the bound.
No kernel may reach another device: no remote copies, remote signals or barrier semaphores. Data moves between devices by JAX's collectives and lax.ppermute only.
A program may use at most 64 MiB of HBM per device.

v0:
```python
import jax
import jax.numpy as jnp
from jax import lax
from jax.sharding import PartitionSpec as P

NV = 16
NC = 16
S = 2


def split_up(shard, dim, length):
    lengths = shard.shape
    tiles = shard.reshape(*lengths[:dim], length, lengths[dim] // length, *lengths[dim + 1 :])
    return jnp.moveaxis(tiles, dim, 0)


def sum_at_owner(shard, axis, dim):
    length = lax.axis_size(axis)
    tiles = lax.all_to_all(split_up(shard, dim, length), axis, 0, 0, tiled=True)
    return jnp.sum(tiles.astype(jnp.float32), axis=0)


def from_behind(value, axis, steps):
    count = lax.axis_size(axis)
    pairs = [(source, (source + steps) % count) for source in range(count)]
    return lax.ppermute(value, axis, pairs)


def pair_fields(left_bands, right_bands, fitting):
    products = (
        left_bands.astype(jnp.float32)[:, None, :] * right_bands.astype(jnp.float32)[None, :, :]
    ).astype(jnp.bfloat16)
    flat = products.reshape(left_bands.shape[0] * right_bands.shape[0], left_bands.shape[1])
    return jnp.dot(flat, fitting, preferred_element_type=jnp.float32).astype(jnp.bfloat16)


def shards(orbitals, fitting, screen, coulomb, qindex):
    per_dev = orbitals.shape[0]
    pair_count = lax.axis_size("pair")
    pair_index = lax.axis_index("pair")
    loop_index = lax.axis_index("kloop")
    slice_width = screen.shape[2]
    val_rows = NV // pair_count
    fitting_part = lax.dynamic_slice_in_dim(fitting, pair_index * slice_width, slice_width, 1)

    def column_fields(orbital):
        return pair_fields(orbital[:NV], orbital[NV:], fitting)

    stacked = []
    own_fields = [column_fields(orbitals[local_k]) for local_k in range(per_dev)]
    for shift_step in range(1, S + 1):
        arrived = from_behind(orbitals, "kloop", -shift_step)
        blocks = []
        for local_k in range(per_dev):
            column = loop_index * per_dev + local_k
            row_orbital = arrived[local_k]
            row_chosen = lax.dynamic_slice_in_dim(
                row_orbital[:NV], pair_index * val_rows, val_rows, 0
            )
            row_fields = pair_fields(row_chosen, row_orbital[NV:], fitting)
            row_orb = arrived[local_k]
            col_orb = orbitals[local_k]
            q_pick = qindex[column, shift_step - 1]
            interaction = lax.dynamic_index_in_dim(screen, q_pick, 0, keepdims=False)
            vale = pair_fields(row_orb[:NV], col_orb[:NV], fitting_part).reshape(
                NV, NV, slice_width
            )
            cond = pair_fields(row_orb[NV:], col_orb[NV:], fitting)
            screened = jnp.dot(cond, interaction, preferred_element_type=jnp.float32)
            screened = screened.astype(jnp.bfloat16).reshape(NC, NC, slice_width)
            terms = jnp.einsum("xyg,vwg->vxwy", screened, vale, preferred_element_type=jnp.float32)
            direct = sum_at_owner(
                terms.reshape(val_rows * NC * lax.axis_size("pair"), NV * NC).astype(jnp.bfloat16),
                "pair",
                0,
            )
            exchange = lax.dot_general(
                (row_fields.astype(jnp.float32) * coulomb).astype(jnp.bfloat16),
                own_fields[local_k],
                (((1,), (1,)), ((), ())),
                preferred_element_type=jnp.float32,
            )
            blocks.append((2.0 * exchange - direct).astype(jnp.bfloat16))
        stacked.append(jnp.stack(blocks, 0))
    return jnp.stack(stacked, axis=1)


def solution(mesh):
    return jax.shard_map(
        shards,
        mesh=mesh,
        in_specs=(P("kloop", None, None), P(), P(None, None, "pair"), P(), P()),
        out_specs=P("kloop", None, "pair", None),
        check_vma=False,
    )
```

profile of v0, /device:TPU:1, one launch (start us, length us, event | category | flops | bytes accessed | tf_op | source)
XLA Modules:
  0.0 130.9 jit_solution(14435675423004822319)
XLA Ops:
  0.0 24.8 %collective-permute-start = (bf16[2,32,512]{2,1,0:T(8,128)(2,1)}, bf16[2,32,512]{2,1,0:T(8,128)(2,1)}, u32[]{:S(2)}, u32[]{:S(2)}) collective-permute-start(bf16[2,32,512]{2,1,0:T(8,128)(2,1)} %param.5), channel_id=1, source_target_pairs={{0,1020},{4,0},{8,4},{12,8},{16,12},{20,16},{24,20},{28,24},{32,28... | collective-permute-start | bytes 196616 | tf_op jit(solution)/shard_map/ppermute | solution.py:26
  24.8 2.4 %collective-permute-start.1 = (bf16[2,32,512]{2,1,0:T(8,128)(2,1)}, bf16[2,32,512]{2,1,0:T(8,128)(2,1)}, u32[]{:S(2)}, u32[]{:S(2)}) collective-permute-start(bf16[2,32,512]{2,1,0:T(8,128)(2,1)} %param.5), channel_id=1, source_target_pairs={{0,1016},{4,1020},{8,0},{12,4},{16,8},{20,12},{24,16},{28,20},{32,... | collective-permute-start | bytes 196616 | tf_op jit(solution)/shard_map/ppermute | solution.py:26
  27.2 1.5 %constant_dynamic-slice_fusion.5 = (s32[1,1]{0,1:T(1,128)}, s32[1,1]{0,1:T(1,128)}, s32[1,1]{0,1:T(1,128)}, s32[1,1]{0,1:T(1,128)}) fusion(s32[512,2]{0,1:T(2,128)} %param.9, s32[]{:T(128)S(6)} %select_n.32, s32[]{:T(128)S(6)} %select_n.34), kind=kLoop, calls=%fused_computation.123 | loop fusion | bytes 40 | tf_op jit(solution)/shard_map/dynamic_slice | solution.py:63
  36.3 15.2 %constant_dynamic-slice_fusion.4 = (bf16[1,1400,350]{1,0,2:T(2,128)(2,1)}, bf16[1,1400,350]{1,0,2:T(2,128)(2,1)}, bf16[1,1400,350]{1,0,2:T(2,128)(2,1)}, bf16[1,1400,350]{1,0,2:T(2,128)(2,1)S(1)}) fusion(bf16[4,1400,350]{1,0,2:T(4,128)(2,1)} %param.7, s32[]{:T(128)S(6)} %select_n.33, s32[]{:T(128)S(6)} %select_n.36, s32[]{:T(128)S(6)} %select_n.35, ...), kind=kLoop, calls=%fused_computation.122 | loop fusion | bytes 7840016 | tf_op jit(solution)/shard_map/jit(dynamic_index_in_dim)/dynamic_slice | solution.py:64
  52.2 1.4 %fusion.60 = (bf16[1,16,512]{2,1,0:T(8,128)(2,1)S(1)}, f32[16,512]{1,0:T(8,128)S(1)}, f32[16,512]{1,0:T(8,128)S(1)}, f32[16,512]{1,0:T(8,128)S(1)}, bf16[1,16,512]{2,1,0:T(8,128)(2,1)}, /*index=5*/f32[16,512]{1,0:T(8,128)S(1)}) fusion(bf16[2,32,512]{2,1,0:T(8,128)(2,1)} %collective-permute-done), kind=kLoop, calls=%fused_computation.127 | loop fusion | flops 32768 | bytes 229376 | tf_op jit(solution)/shard_map/slice | solution.py:58
  53.6 1.4 %fusion.61 = (bf16[1,16,512]{2,1,0:T(8,128)(2,1)}, f32[16,512]{1,0:T(8,128)S(1)}, f32[16,512]{1,0:T(8,128)S(1)}, f32[16,512]{1,0:T(8,128)S(1)}, bf16[1,16,512]{2,1,0:T(8,128)(2,1)}, /*index=5*/f32[16,512]{1,0:T(8,128)S(1)}) fusion(bf16[2,32,512]{2,1,0:T(8,128)(2,1)} %collective-permute-done.1), kind=kLoop, calls=%fused_computation.128 | loop fusion | flops 32768 | bytes 229376 | tf_op jit(solution)/shard_map/slice | solution.py:58
  55.0 2.5 %multiply_convert_fusion.4 = (bf16[16,16,512]{2,1,0:T(8,128)(2,1)}, bf16[16,16,512]{2,1,0:T(8,128)(2,1)}, bf16[16,16,512]{2,1,0:T(8,128)(2,1)}, bf16[16,16,512]{...) fusion(f32[16,512]{1,0:T(8,128)S(1)} %get-tuple-element.12, ...), kind=kLoop, calls=%fused_computation.70 | loop fusion | flops 2621440 | bytes 3014656 | tf_op jit(solution)/shard_map/convert_element_type | solution.py:32
  57.5 1.0 convolution_convert_fusion.14
  58.4 1.7 %copy.24 = bf16[256,350]{1,0:T(8,128)(2,1)} copy(bf16[256,350]{0,1:T(8,128)(2,1)} %convolution_convert_fusion.14) | data formatting | bytes 358400 | tf_op jit(solution)/shard_map/convert_element_type | solution.py:34
  60.2 2.5 %fusion.20 = bf16[256,350]{0,1:T(8,128)(2,1)} fusion(bf16[256,512]{1,0:T(8,128)(2,1)} %bitcast.191, bf16[512,1400]{0,1:T(8,128)(2,1)S(1)} %copy-done, bf16[1,1400,350]{1,0,2:T(2,128)(2,1)S(1)} %get-tuple-element.8), kind=kOutput, calls=%fused_computation.34 | convolution fusion | flops 618329600 | bytes 2854944 | tf_op jit(solution)/shard_map/dot_general | solution.py:69
  62.7 1.1 copy.26
  63.8 1.7 %fusion.15 = bf16[16,16,16,16]{3,2,1,0:T(8,128)(2,1)S(1)} fusion(bf16[16,16,350,1]{2,1,3,0:T(8,128)(2,1)} %bitcast.197, bf16[16,16,350,1]{2,1,0,3:T(8,128)(2,1)S(1)} %bitcast.200), kind=kOutput, calls=%fused_computation.29 | convolution fusion | flops 45940736 | bytes 489472 | tf_op jit(solution)/shard_map/xyg,vwg->vxwy/dot_general | solution.py:71
  65.5 1.7 %convert_element_type.477 = bf16[4,64,256]{2,1,0:T(8,128)(2,1)} reshape(bf16[16,16,16,16]{3,2,1,0:T(8,128)(2,1)S(1)} %fusion.15) | data formatting | bytes 262144 | tf_op jit(solution)/shard_map/convert_element_type | solution.py:73
  67.2 4.7 %all-to-all-start.3 = ((bf16[4,64,256]{2,1,0:T(8,128)(2,1)}), bf16[4,64,256]{2,1,0:T(8,128)(2,1)S(1)}, u32[]{:S(2)}, u32[]{:S(2)}) async-start(bf16[4,64,256]{2,1,0:T(8,128)(2,1)} %convert_element_type.477), calls=%async_computation.3 | async-start | bytes 262144 | tf_op jit(solution)/shard_map/all_to_all | solution.py:19
  74.3 2.5 %fusion.21 = bf16[256,350]{0,1:T(8,128)(2,1)S(1)} fusion(bf16[256,512]{1,0:T(8,128)(2,1)S(1)} %bitcast.190, bf16[512,1400]{0,1:T(8,128)(2,1)S(1)} %copy-done, bf16[1,1400,350]{1,0,2:T(2,128)(2,1)} %get-tuple-element.6), kind=kOutput, calls=%fused_computation.35 | convolution fusion | flops 618329600 | bytes 2854944 | tf_op jit(solution)/shard_map/dot_general | solution.py:69
  76.9 1.7 %fusion.14 = bf16[16,16,16,16]{3,2,1,0:T(8,128)(2,1)} fusion(bf16[16,16,350,1]{2,1,3,0:T(8,128)(2,1)S(1)} %bitcast.198, bf16[16,16,350,1]{2,1,0,3:T(8,128)(2,1)S(1)} %bitcast.201), kind=kOutput, calls=%fused_computation.28 | convolution fusion | flops 45940736 | bytes 489472 | tf_op jit(solution)/shard_map/xyg,vwg->vxwy/dot_general | solution.py:71
  78.6 2.8 %convert_element_type.456 = bf16[4,64,256]{2,1,0:T(8,128)(2,1)} reshape(bf16[16,16,16,16]{3,2,1,0:T(8,128)(2,1)} %fusion.14) | data formatting | bytes 262144 | tf_op jit(solution)/shard_map/convert_element_type | solution.py:73
  83.1 0.8 copy.18
  83.9 2.5 %fusion.22 = bf16[256,350]{0,1:T(8,128)(2,1)S(1)} fusion(bf16[256,512]{1,0:T(8,128)(2,1)} %bitcast.189, bf16[512,1400]{0,1:T(8,128)(2,1)S(1)} %copy-done, bf16[1,1400,350]{1,0,2:T(2,128)(2,1)} %get-tuple-element.7), kind=kOutput, calls=%fused_computation.36 | convolution fusion | flops 618329600 | bytes 2854944 | tf_op jit(solution)/shard_map/dot_general | solution.py:69
  86.5 0.8 copy.20
  87.3 2.7 %fusion.13 = bf16[16,16,16,16]{3,2,1,0:T(8,128)(2,1)} fusion(bf16[16,16,350,1]{2,1,3,0:T(8,128)(2,1)} %bitcast.199, bf16[16,16,350,1]{2,1,0,3:T(8,128)(2,1)} %bitcast.202), kind=kOutput, calls=%fused_computation.27 | convolution fusion | flops 45940736 | bytes 489472 | tf_op jit(solution)/shard_map/xyg,vwg->vxwy/dot_general | solution.py:71
  90.0 2.8 %convert_element_type.435 = bf16[4,64,256]{2,1,0:T(8,128)(2,1)} reshape(bf16[16,16,16,16]{3,2,1,0:T(8,128)(2,1)} %fusion.13) | data formatting | bytes 262144 | tf_op jit(solution)/shard_map/convert_element_type | solution.py:73
  95.3 3.2 %fusion.23 = bf16[256,350]{0,1:T(8,128)(2,1)} fusion(bf16[256,512]{1,0:T(8,128)(2,1)} %bitcast.188, bf16[512,1400]{0,1:T(8,128)(2,1)S(1)} %copy-done, bf16[1,1400,350]{1,0,2:T(2,128)(2,1)} %get-tuple-element.5), kind=kOutput, calls=%fused_computation.37 | convolution fusion | flops 618329600 | bytes 2854944 | tf_op jit(solution)/shard_map/dot_general | solution.py:69
  98.6 1.7 %copy.17 = bf16[256,350]{1,0:T(8,128)(2,1)} copy(bf16[256,350]{0,1:T(8,128)(2,1)} %fusion.23) | data formatting | bytes 358400 | tf_op jit(solution)/shard_map/convert_element_type | solution.py:70
  100.3 2.7 %fusion.12 = bf16[16,16,16,16]{3,2,1,0:T(8,128)(2,1)} fusion(bf16[16,16,350,1]{2,1,3,0:T(8,128)(2,1)S(1)} %bitcast.196, bf16[16,16,350,1]{2,1,0,3:T(8,128)(2,1)} %bitcast.203), kind=kOutput, calls=%fused_computation.26 | convolution fusion | flops 45940736 | bytes 489472 | tf_op jit(solution)/shard_map/xyg,vwg->vxwy/dot_general | solution.py:71
  103.0 2.8 %convert_element_type.409 = bf16[4,64,256]{2,1,0:T(8,128)(2,1)} reshape(bf16[16,16,16,16]{3,2,1,0:T(8,128)(2,1)} %fusion.12) | data formatting | bytes 262144 | tf_op jit(solution)/shard_map/convert_element_type | solution.py:73
  106.5 3.5 %all-to-all-start.2 = ((bf16[4,64,256]{2,1,0:T(8,128)(2,1)}), bf16[4,64,256]{2,1,0:T(8,128)(2,1)S(1)}, u32[]{:S(2)}, u32[]{:S(2)}) async-start(bf16[4,64,256]{2,1,0:T(8,128)(2,1)} %convert_element_type.456), calls=%async_computation.2 | async-start | bytes 262144 | tf_op jit(solution)/shard_map/all_to_all | solution.py:19
  110.9 2.7 %all-to-all-done.2 = bf16[4,64,256]{2,1,0:T(8,128)(2,1)S(1)} async-done(((bf16[4,64,256]{2,1,0:T(8,128)(2,1)}), bf16[4,64,256]{2,1,0:T(8,128)(2,1)S(1)}, u32[]{:S(2)}, u32[]{:S(2)}) %all-to-all-start.2) | async-done | bytes 131104 | tf_op jit(solution)/shard_map/all_to_all | solution.py:19
  113.6 4.3 %all-to-all-start.1 = ((bf16[4,64,256]{2,1,0:T(8,128)(2,1)}), bf16[4,64,256]{2,1,0:T(8,128)(2,1)S(1)}, u32[]{:S(2)}, u32[]{:S(2)}) async-start(bf16[4,64,256]{2,1,0:T(8,128)(2,1)} %convert_element_type.435), calls=%async_computation.1 | async-start | bytes 262144 | tf_op jit(solution)/shard_map/all_to_all | solution.py:19
  118.8 2.7 %all-to-all-done.1 = bf16[4,64,256]{2,1,0:T(8,128)(2,1)S(1)} async-done(((bf16[4,64,256]{2,1,0:T(8,128)(2,1)}), bf16[4,64,256]{2,1,0:T(8,128)(2,1)S(1)}, u32[]{:S(2)}, u32[]{:S(2)}) %all-to-all-start.1) | async-done | bytes 131104 | tf_op jit(solution)/shard_map/all_to_all | solution.py:19
  121.5 4.3 %all-to-all-start = ((bf16[4,64,256]{2,1,0:T(8,128)(2,1)}), bf16[4,64,256]{2,1,0:T(8,128)(2,1)S(1)}, u32[]{:S(2)}, u32[]{:S(2)}) async-start(bf16[4,64,256]{2,1,0:T(8,128)(2,1)} %convert_element_type.409), calls=%async_computation | async-start | bytes 262144 | tf_op jit(solution)/shard_map/all_to_all | solution.py:19
  126.6 2.7 %all-to-all-done = bf16[4,64,256]{2,1,0:T(8,128)(2,1)S(1)} async-done(((bf16[4,64,256]{2,1,0:T(8,128)(2,1)}), bf16[4,64,256]{2,1,0:T(8,128)(2,1)S(1)}, u32[]{:S(2)}, u32[]{:S(2)}) %all-to-all-start) | async-done | bytes 131104 | tf_op jit(solution)/shard_map/all_to_all | solution.py:19
  (66 shorter events, 12.0 us)
Async XLA Ops:
  0.0 57.4 %copy-start = (bf16[512,1400]{0,1:T(8,128)(2,1)S(1)}, bf16[512,1400]{0,1:T(8,128)(2,1)}, u32[]{:S(2)}) copy-start(bf16[512,1400]{0,1:T(8,128)(2,1)} %param.6) | copy-start | bytes 4300804
  0.0 52.2 %collective-permute-start = (bf16[2,32,512]{2,1,0:T(8,128)(2,1)}, bf16[2,32,512]{2,1,0:T(8,128)(2,1)}, u32[]{:S(2)}, u32[]{:S(2)}) collective-permute-start(bf16[2,32,512]{2,1,0:T(8,128)(2,1)} %param.5), channel_id=1, source_target_pairs={{0,1020},{4,0},{8,4},{12,8},{16,12},{20,16},{24,20},{28,24},{32,28... | collective-permute-start | bytes 196616 | tf_op jit(solution)/shard_map/ppermute | solution.py:26
  24.8 28.8 %collective-permute-start.1 = (bf16[2,32,512]{2,1,0:T(8,128)(2,1)}, bf16[2,32,512]{2,1,0:T(8,128)(2,1)}, u32[]{:S(2)}, u32[]{:S(2)}) collective-permute-start(bf16[2,32,512]{2,1,0:T(8,128)(2,1)} %param.5), channel_id=1, source_target_pairs={{0,1016},{4,1020},{8,0},{12,4},{16,8},{20,12},{24,16},{28,20},{32,... | collective-permute-start | bytes 196616 | tf_op jit(solution)/shard_map/ppermute | solution.py:26
  36.3 15.2 %copy-start.17 = (bf16[2,32,512]{2,1,0:T(8,128)(2,1)S(1)}, bf16[2,32,512]{2,1,0:T(8,128)(2,1)}, u32[]{:S(2)}) copy-start(bf16[2,32,512]{2,1,0:T(8,128)(2,1)} %param.5) | copy-start | bytes 196612
  55.0 2.5 %copy-start.6 = (f32[16,512]{1,0:T(8,128)}, f32[16,512]{1,0:T(8,128)S(1)}, u32[]{:S(2)}) copy-start(f32[16,512]{1,0:T(8,128)S(1)} %get-tuple-element.20) | copy-start | bytes 98308
  55.0 2.5 %copy-start.8 = (f32[16,512]{1,0:T(8,128)}, f32[16,512]{1,0:T(8,128)S(1)}, u32[]{:S(2)}) copy-start(f32[16,512]{1,0:T(8,128)S(1)} %get-tuple-element.18) | copy-start | bytes 98308
  63.8 8.1 %copy-start.2 = (bf16[16,16,512]{2,1,0:T(8,128)(2,1)S(1)}, bf16[16,16,512]{2,1,0:T(8,128)(2,1)}, u32[]{:S(2)}) copy-start(bf16[16,16,512]{2,1,0:T(8,128)(2,1)} %get-tuple-element.32) | copy-start | bytes 786436
  67.2 6.0 %copy-start.9 = (f32[16,512]{1,0:T(8,128)S(1)}, f32[16,512]{1,0:T(8,128)}, u32[]{:S(2)}) copy-start(f32[16,512]{1,0:T(8,128)} %copy-done.8) | copy-start | bytes 98308
  67.2 6.6 %copy-start.5 = (bf16[16,16,512]{2,1,0:T(8,128)(2,1)S(1)}, bf16[16,16,512]{2,1,0:T(8,128)(2,1)}, u32[]{:S(2)}) copy-start(bf16[16,16,512]{2,1,0:T(8,128)(2,1)} %get-tuple-element.39) | copy-start | bytes 786436
  67.2 39.3 %all-to-all-start.3 = ((bf16[4,64,256]{2,1,0:T(8,128)(2,1)}), bf16[4,64,256]{2,1,0:T(8,128)(2,1)S(1)}, u32[]{:S(2)}, u32[]{:S(2)}) async-start(bf16[4,64,256]{2,1,0:T(8,128)(2,1)} %convert_element_type.477), calls=%async_computation.3 | async-start | bytes 262144 | tf_op jit(solution)/shard_map/all_to_all | solution.py:19
  71.8 2.4 %copy-start.10 = (bf16[16,16,512]{2,1,0:T(8,128)(2,1)S(1)}, bf16[16,16,512]{2,1,0:T(8,128)(2,1)}, u32[]{:S(2)}) copy-start(bf16[16,16,512]{2,1,0:T(8,128)(2,1)} %get-tuple-element.42) | copy-start | bytes 786436
  76.9 4.5 %copy-start.1 = (bf16[16,16,512]{2,1,0:T(8,128)(2,1)S(1)}, bf16[16,16,512]{2,1,0:T(8,128)(2,1)}, u32[]{:S(2)}) copy-start(bf16[16,16,512]{2,1,0:T(8,128)(2,1)} %get-tuple-element.41) | copy-start | bytes 786436
  81.4 0.8 copy-start.7
  81.4 1.4 %copy-start.4 = (bf16[16,16,512]{2,1,0:T(8,128)(2,1)S(1)}, bf16[16,16,512]{2,1,0:T(8,128)(2,1)}, u32[]{:S(2)}) copy-start(bf16[16,16,512]{2,1,0:T(8,128)(2,1)} %get-tuple-element.33) | copy-start | bytes 786436
  87.3 6.9 %copy-start.3 = (bf16[16,16,512]{2,1,0:T(8,128)(2,1)S(1)}, bf16[16,16,512]{2,1,0:T(8,128)(2,1)}, u32[]{:S(2)}) copy-start(bf16[16,16,512]{2,1,0:T(8,128)(2,1)} %get-tuple-element.40) | copy-start | bytes 786436
  95.3 5.0 %copy-start.15 = (bf16[256,350]{1,0:T(8,128)(2,1)S(1)}, bf16[256,350]{1,0:T(8,128)(2,1)}, u32[]{:S(2)}) copy-start(bf16[256,350]{1,0:T(8,128)(2,1)} %copy.15) | copy-start | bytes 537604
  100.3 9.7 %copy-start.11 = (bf16[4,16,512]{2,1,0:T(8,128)(2,1)S(1)}, bf16[4,16,512]{2,1,0:T(8,128)(2,1)}, u32[]{:S(2)}) copy-start(bf16[4,16,512]{2,1,0:T(8,128)(2,1)} %multiply_convert_fusion.10) | copy-start | bytes 196612
  100.3 9.7 %copy-start.16 = (f32[1400]{0:T(1024)S(1)}, f32[1400]{0:T(1024)}, u32[]{:S(2)}) copy-start(f32[1400]{0:T(1024)} %param.8) | copy-start | bytes 16804
  106.5 7.1 %all-to-all-start.2 = ((bf16[4,64,256]{2,1,0:T(8,128)(2,1)}), bf16[4,64,256]{2,1,0:T(8,128)(2,1)S(1)}, u32[]{:S(2)}, u32[]{:S(2)}) async-start(bf16[4,64,256]{2,1,0:T(8,128)(2,1)} %convert_element_type.456), calls=%async_computation.2 | async-start | bytes 262144 | tf_op jit(solution)/shard_map/all_to_all | solution.py:19
  110.0 7.9 %copy-start.12 = (bf16[4,16,512]{2,1,0:T(8,128)(2,1)S(1)}, bf16[4,16,512]{2,1,0:T(8,128)(2,1)}, u32[]{:S(2)}) copy-start(bf16[4,16,512]{2,1,0:T(8,128)(2,1)} %multiply_convert_fusion.11) | copy-start | bytes 196612
  113.6 7.9 %all-to-all-start.1 = ((bf16[4,64,256]{2,1,0:T(8,128)(2,1)}), bf16[4,64,256]{2,1,0:T(8,128)(2,1)S(1)}, u32[]{:S(2)}, u32[]{:S(2)}) async-start(bf16[4,64,256]{2,1,0:T(8,128)(2,1)} %convert_element_type.435), calls=%async_computation.1 | async-start | bytes 262144 | tf_op jit(solution)/shard_map/all_to_all | solution.py:19
  117.9 7.9 %copy-start.13 = (bf16[4,16,512]{2,1,0:T(8,128)(2,1)S(1)}, bf16[4,16,512]{2,1,0:T(8,128)(2,1)}, u32[]{:S(2)}) copy-start(bf16[4,16,512]{2,1,0:T(8,128)(2,1)} %multiply_convert_fusion.12) | copy-start | bytes 196612
  118.8 10.6 %copy-start.14 = (bf16[4,16,512]{2,1,0:T(8,128)(2,1)S(1)}, bf16[4,16,512]{2,1,0:T(8,128)(2,1)}, u32[]{:S(2)}) copy-start(bf16[4,16,512]{2,1,0:T(8,128)(2,1)} %multiply_convert_fusion.13) | copy-start | bytes 196612
  121.5 7.9 %all-to-all-start = ((bf16[4,64,256]{2,1,0:T(8,128)(2,1)}), bf16[4,64,256]{2,1,0:T(8,128)(2,1)S(1)}, u32[]{:S(2)}, u32[]{:S(2)}) async-start(bf16[4,64,256]{2,1,0:T(8,128)(2,1)} %convert_element_type.409), calls=%async_computation | async-start | bytes 262144 | tf_op jit(solution)/shard_map/all_to_all | solution.py:19
where the time goes:
time: 132 us; the launch traced here: 131 us
  starting transfers between devices  44.1 us (33%)
  local copies, waits for them, and re-layouts  35.1 us (27%)
  matrix products  25.8 us (20%)
  other arithmetic  9.93 us (8%)
  waiting for transfers between devices  8.14 us (6%)
  between operations  7.89 us (6%)
    ppermute x2, starting transfers between devices, from_behind(): return lax.ppermute(value, axis, pairs)  27.2 us
    all_to_all x4, starting transfers between devices, sum_at_owner(): tiles = lax.all_to_all(split_up(shard, dim, length), axis, 0, 0, tiled=True)  16.9 us
    dynamic_slice x1, local copies, waits for them, and re-layouts, shards(): interaction = lax.dynamic_index_in_dim(screen, q_pick, 0, keepdims=False)  15.2 us
    dot_general x4, matrix products, shards(): screened = jnp.dot(cond, interaction, preferred_element_type=jnp.float32)  10.8 us
    convert_element_type x4, local copies, waits for them, and re-layouts, shards(): terms.reshape(val_rows * NC * lax.axis_size('pair'), NV * NC)  10.2 us
    dot_general x4, matrix products, shards(): jnp.einsum('xyg,vwg->vxwy', screened, vale, preferred_element_type=jnp.fl...  8.76 us
    all_to_all x4, waiting for transfers between devices, sum_at_owner(): tiles = lax.all_to_all(split_up(shard, dim, length), axis, 0, 0, tiled=True)  8.13 us
    convert_element_type x5, other arithmetic, pair_fields(): products = (left_bands.astype(jnp.float32)[:, None, :] * right_bands.asty...  4.99 us
  transfers between devices with their start and end apart: 6, of which 3 were waited for; matrix products, arithmetic and copies ran while one was open for 42% of the time, Pallas kernels for 0%

commit v1 on v0

v1 whole, which is shorter than its diff:
```python
import jax
import jax.numpy as jnp
from jax import lax
from jax.sharding import PartitionSpec as P

NV = 16
NC = 16
S = 2


def from_behind(value, axis, steps):
    count = lax.axis_size(axis)
    pairs = [(source, (source + steps) % count) for source in range(count)]
    return lax.ppermute(value, axis, pairs)


def products(left_bands, right_bands):
    prod = left_bands.astype(jnp.float32)[..., :, None, :] * right_bands.astype(jnp.float32)[..., None, :, :]
    lead = prod.shape[:-3]
    return prod.astype(jnp.bfloat16).reshape(*lead, prod.shape[-3] * prod.shape[-2], prod.shape[-1])


def fields(left_bands, right_bands, fit):
    prod = products(left_bands, right_bands)
    return jnp.einsum("...pm,mg->...pg", prod, fit, preferred_element_type=jnp.float32).astype(jnp.bfloat16)


def shards(orbitals, fitting, screen, coulomb, qindex):
    per_dev = orbitals.shape[0]
    npair = lax.axis_size("pair")
    pair_index = lax.axis_index("pair")
    loop_index = lax.axis_index("kloop")
    width = screen.shape[2]
    ng = screen.shape[1]
    vr = NV // npair
    fitting_part = lax.dynamic_slice_in_dim(fitting, pair_index * width, width, 1)

    rows = jnp.stack([from_behind(orbitals, "kloop", -s) for s in range(1, S + 1)], 0)
    cols = jnp.broadcast_to(orbitals[None], rows.shape)

    own = fields(orbitals[:, :NV], orbitals[:, NV:], fitting)

    cond = fields(rows[:, :, NV:], cols[:, :, NV:], fitting)
    vale = fields(rows[:, :, :NV], cols[:, :, :NV], fitting_part)

    screen2d = screen.reshape(screen.shape[0] * ng, width)
    screened = []
    for s in range(S):
        row_s = []
        for lk in range(per_dev):
            q = qindex[loop_index * per_dev + lk, s]
            inter = lax.dynamic_slice_in_dim(screen2d, q * ng, ng, 0)
            row_s.append(jnp.dot(cond[s, lk], inter, preferred_element_type=jnp.float32).astype(jnp.bfloat16))
        screened.append(jnp.stack(row_s, 0))
    screened = jnp.stack(screened, 0)

    terms = jnp.einsum("abpg,abqg->abpq", vale, screened, preferred_element_type=jnp.float32).astype(jnp.bfloat16)
    terms = terms.reshape(S, per_dev, npair, vr * NV, NC * NC)
    terms = jnp.moveaxis(terms, 2, 0)
    got = lax.all_to_all(terms, "pair", 0, 0, tiled=True)
    dsum = jnp.sum(got.astype(jnp.float32), axis=0)
    direct = dsum.reshape(S, per_dev, vr, NV, NC, NC).transpose(0, 1, 2, 4, 3, 5).reshape(S, per_dev, vr * NC, NV * NC)

    row_chosen = lax.dynamic_slice_in_dim(rows, pair_index * vr, vr, 2)
    rowf = fields(row_chosen, rows[:, :, NV:], fitting)
    weighted = (rowf.astype(jnp.float32) * coulomb).astype(jnp.bfloat16)
    exchange = jnp.einsum("abpg,bqg->abpq", weighted, own, preferred_element_type=jnp.float32)
    out = (2.0 * exchange - direct).astype(jnp.bfloat16)
    return jnp.swapaxes(out, 0, 1)


def solution(mesh):
    return jax.shard_map(
        shards,
        mesh=mesh,
        in_specs=(P("kloop", None, None), P(), P(None, None, "pair"), P(), P()),
        out_specs=P("kloop", None, "pair", None),
        check_vma=False,
    )
```

time: 132 us -> 71 us (0.54)
  local copies, waits for them, and re-layouts: 35.1 us -> 17 us
  matrix products: 25.8 us -> 9.3 us
  starting transfers between devices: 44.1 us -> 31.9 us
  other arithmetic: 9.93 us -> 4.55 us
  between operations: 7.89 us -> 2.72 us
  waiting for transfers between devices: 8.14 us -> 4.96 us
    convert_element_type x12 -> x0, local copies, waits for them, and re-layouts: 17.5 us -> none  [the longest x4 10.2 us: shards(): terms.reshape(val_rows * NC * lax.axis_size('pair'), NV * NC)]
    dot_general x18 -> x8, matrix products: 25.8 us -> 9.3 us  [the longest x2 3.75 us: fields(): jnp.einsum('...pm,mg->...pg', prod, fit, preferred_element_type=jnp.float32)]
    dynamic_slice x2 -> x1, local copies, waits for them, and re-layouts: 16.7 us -> 1.49 us  [shards(): q = qindex[loop_index * per_dev + lk, s]]
    reshape x0 -> x4, local copies, waits for them, and re-layouts: none -> 12.9 us  [the longest x1 7.8 us: shards(): screen2d = screen.reshape(screen.shape[0] * ng, width)]
    all_to_all x4 -> x1, starting transfers between devices: 16.9 us -> 4.67 us  [shards(): got = lax.all_to_all(terms, 'pair', 0, 0, tiled=True)]
    convert_element_type x7 -> x5, other arithmetic: 6.42 us -> 2.21 us  [the longest x3 1.37 us: products(): prod.astype(jnp.bfloat16)]
    all_to_all x4 -> x1, waiting for transfers between devices: 8.13 us -> 4.95 us  [shards(): got = lax.all_to_all(terms, 'pair', 0, 0, tiled=True)]
    slice x2 -> x0, other arithmetic: 2.76 us -> none  [shards(): row_orbital[:NV]]
  transfers between devices with their start and end apart: 6 -> 3, of which waited for: 3 -> 1; matrix products, arithmetic and copies ran while one was open for 42% -> 18% of each run, Pallas kernels for 0% -> 0%
where the time goes in v1:
time: 71 us; the launch traced here: 70.4 us
  starting transfers between devices  31.9 us (45%)
  local copies, waits for them, and re-layouts  17 us (24%)
  matrix products  9.3 us (13%)
  waiting for transfers between devices  4.96 us (7%)
  other arithmetic  4.55 us (6%)
  between operations  2.72 us (4%)
    ppermute x2, starting transfers between devices, from_behind(): return lax.ppermute(value, axis, pairs)  27.2 us
    reshape x1, local copies, waits for them, and re-layouts, shards(): screen2d = screen.reshape(screen.shape[0] * ng, width)  7.8 us
    all_to_all x1, waiting for transfers between devices, shards(): got = lax.all_to_all(terms, 'pair', 0, 0, tiled=True)  4.95 us
    all_to_all x1, starting transfers between devices, shards(): got = lax.all_to_all(terms, 'pair', 0, 0, tiled=True)  4.67 us
    reshape x2, local copies, waits for them, and re-layouts, shards(): dsum.reshape(S, per_dev, vr, NV, NC, NC).transpose(0, 1, 2, 4, 3, 5)  4.23 us
    dot_general x2, matrix products, fields(): jnp.einsum('...pm,mg->...pg', prod, fit, preferred_element_type=jnp.float32)  3.75 us
    dot_general x4, matrix products, shards(): jnp.dot(cond[s, lk], inter, preferred_element_type=jnp.float32)  2.14 us
    transpose x1, local copies, waits for them, and re-layouts, shards(): dsum.reshape(S, per_dev, vr, NV, NC, NC).transpose(0, 1, 2, 4, 3, 5)  2 us
  transfers between devices with their start and end apart: 3, of which 1 were waited for; matrix products, arithmetic and copies ran while one was open for 18% of the time, Pallas kernels for 0%

profile of v1, /device:TPU:1, one launch (start us, length us, event | category | flops | bytes accessed | tf_op | source)
XLA Modules:
  0.0 70.4 jit_solution(2627114727336293815)
XLA Ops:
  0.0 24.8 %collective-permute-start = (bf16[2,32,512]{2,1,0:T(8,128)(2,1)}, bf16[2,32,512]{2,1,0:T(8,128)(2,1)S(1)}, u32[]{:S(2)}, u32[]{:S(2)}) collective-permute-start(bf16[2,32,512]{2,1,0:T(8,128)(2,1)} %param.5), channel_id=1, source_target_pairs={{0,1020},{4,0},{8,4},{12,8},{16,12},{20,16},{24,20},{28,24},{32,28... | collective-permute-start | bytes 196616 | tf_op jit(solution)/shard_map/ppermute | solution.py:14
  24.8 2.4 %collective-permute-start.1 = (bf16[2,32,512]{2,1,0:T(8,128)(2,1)}, bf16[2,32,512]{2,1,0:T(8,128)(2,1)S(1)}, u32[]{:S(2)}, u32[]{:S(2)}) collective-permute-start(bf16[2,32,512]{2,1,0:T(8,128)(2,1)} %param.5), channel_id=1, source_target_pairs={{0,1016},{4,1020},{8,0},{12,4},{16,8},{20,12},{24,16},{28,20},{32,... | collective-permute-start | bytes 196616 | tf_op jit(solution)/shard_map/ppermute | solution.py:14
  27.2 0.8 %slice_convert_fusion = (f32[2,16,512]{2,1,0:T(8,128)S(1)}, f32[2,16,512]{2,1,0:T(8,128)S(1)}) fusion(bf16[2,32,512]{2,1,0:T(8,128)(2,1)} %param.5), kind=kLoop, calls=%fused_computation.59 | loop fusion | flops 32768 | bytes 196608 | tf_op jit(solution)/shard_map/convert_element_type | solution.py:18
  28.0 1.5 %constant_dynamic-slice_fusion.1 = (s32[1,1]{0,1:T(1,128)}, s32[1,1]{0,1:T(1,128)}, s32[1,1]{0,1:T(1,128)}, s32[1,1]{0,1:T(1,128)}) fusion(s32[512,2]{0,1:T(2,128)} %param.9, s32[]{:T(128)S(6)} %select_n.28, s32[]{:T(128)S(6)} %select_n.30), kind=kLoop, calls=%fused_computation.68 | loop fusion | bytes 40 | tf_op jit(solution)/shard_map/dynamic_slice | solution.py:51
  32.1 7.8 %reshape.44 = bf16[5600,350]{0,1:T(8,128)(2,1)} reshape(bf16[4,1400,350]{1,0,2:T(4,128)(2,1)} %param.7) | data formatting | bytes 7840000 | tf_op jit(solution)/shard_map/reshape | solution.py:46
  39.9 0.0 collective-permute-done
  39.9 0.0 collective-permute-done.1
  39.9 0.1 mul.124
  40.0 0.1 mul.138
  40.2 0.5 fusion.4
  40.7 1.7 %convolution_convert_fusion = bf16[2,2,256,1400]{2,3,1,0:T(8,128)(2,1)S(1)} fusion(bf16[2,2,256,512]{3,2,1,0:T(8,128)(2,1)S(1)} %get-tuple-element.13, bf16[512,1400]{0,1:T(8,128)(2,1)S(1)} %copy-done), kind=kOutput, calls=%fused_computation | convolution fusion | flops 1469440000 | bytes 5349376 | tf_op jit(solution)/shard_map/...pm,mg->...pg/dot_general | solution.py:25
  42.4 0.4 copy-done.1
  42.9 0.5 fusion.24
  43.4 0.5 fusion.25
  43.9 0.5 fusion.26
  44.5 0.5 fusion.27
  45.0 0.8 %maximum_bitcast_fusion = bf16[1,2,256,350]{2,3,1,0:T(8,128)(2,1)} fusion(bf16[1,256,350]{1,2,0:T(8,128)(2,1)S(1)} %fusion.25, bf16[1,256,350]{1,2,0:T(8,128)(2,1)S(1)} %fusion.24), kind=kLoop, calls=%fused_computation.47 | loop fusion | flops 179200 | bytes 716800 | tf_op jit(solution)/shard_map/stack | solution.py:55
  45.8 0.8 %maximum_bitcast_fusion.1 = bf16[1,2,256,350]{2,3,1,0:T(8,128)(2,1)} fusion(bf16[1,256,350]{1,2,0:T(8,128)(2,1)S(1)} %fusion.27, bf16[1,256,350]{1,2,0:T(8,128)(2,1)S(1)} %fusion.26), kind=kLoop, calls=%fused_computation.48 | loop fusion | flops 179200 | bytes 716800 | tf_op jit(solution)/shard_map/stack | solution.py:55
  46.6 1.9 %convolution_convert_fusion.4 = bf16[2,2,256,256]{3,2,1,0:T(8,128)(2,1)S(1)} fusion(bf16[2,2,256,512]{3,2,1,0:T(8,128)(2,1)S(1)} %get-tuple-element.14, bf16[1,2,256,350]{2,3,1,0:T(8,128)(2,1)} %maximum_bitcast_fusion.1, bf16[1,2,256,350]{2,3,1,0:T(8,128)(2,1)} %maximum_bitcast_fusion, bf16[512,1400]{0,1:T(8,128)(2,1)S(1)} %copy-done, s32[]{:T(128)S(6)} %select_n.27), kind=kOutput, calls=%fused_computation.15 | convolution fusion | flops 551481344 | bytes 2650116 | tf_op jit(solution)/shard_map/abpg,abqg->abpq/dot_general | solution.py:57
  48.5 0.8 %copy.19 = bf16[2,2,4,64,256]{4,3,1,0,2:T(8,128)(2,1)} copy(bf16[2,2,4,64,256]{4,3,2,1,0:T(8,128)(2,1)S(1)} %bitcast.109) | data formatting | bytes 1048576 | tf_op jit(solution)/shard_map/reshape | solution.py:58
  49.3 4.7 %all-to-all-start = ((bf16[4,2,2,64,256]{4,3,2,1,0:T(8,128)(2,1)}), bf16[4,2,2,64,256]{4,3,2,1,0:T(8,128)(2,1)S(1)}, u32[]{:S(2)}, u32[]{:S(2)}) async-start(bf16[4,2,2,64,256]{4,3,2,1,0:T(8,128)(2,1)} %bitcast.105), calls=%async_computation | async-start | bytes 1048576 | tf_op jit(solution)/shard_map/all_to_all | solution.py:60
  54.0 0.1 fusion.31
  54.1 2.1 %fusion = bf16[2,256,1400,1]{1,2,3,0:T(8,128)(2,1)} fusion(bf16[2,256,512]{2,1,0:T(8,128)(2,1)S(1)} %fusion.31, bf16[512,1400]{0,1:T(8,128)(2,1)S(1)} %copy-done), kind=kOutput, calls=%fused_computation.2 | convolution fusion | flops 734720000 | bytes 3391488 | tf_op jit(solution)/shard_map/...pm,mg->...pg/dot_general | solution.py:25
  56.1 0.8 %multiply_convert_fusion = bf16[2,2,4,16,512]{4,3,2,0,1:T(8,128)(2,1)} fusion(s32[]{:T(128)S(6)} %select_n.26, bf16[1,2,32,512]{3,2,1,0:T(8,128)(2,1)S(1)} %bitcast.114, bf16[1,2,32,512]{3,2,1,0:T(8,128)(2,1)S(1)} %bitcast.112, f32[2,2,16,512]{3,2,1,0:T(8,128)S(1)} %get-tuple-element.5), kind=kLoop, calls=%fused_computation.46 | loop fusion | flops 294912 | bytes 524292 | tf_op jit(solution)/shard_map/convert_element_type | solution.py:20
  56.9 5.0 %all-to-all-done = bf16[4,2,2,64,256]{4,3,2,1,0:T(8,128)(2,1)S(1)} async-done(((bf16[4,2,2,64,256]{4,3,2,1,0:T(8,128)(2,1)}), bf16[4,2,2,64,256]{4,3,2,1,0:T(8,128)(2,1)S(1)}, u32[]{:S(2)}, u32[]{:S(2)}) %all-to-all-start) | async-done | bytes 524320 | tf_op jit(solution)/shard_map/all_to_all | solution.py:60
  61.9 0.8 %convert_reduce_fusion = f32[2,2,64,256]{3,2,1,0:T(8,128)} fusion(bf16[4,2,2,64,256]{4,3,2,1,0:T(8,128)(2,1)S(1)} %all-to-all-done), kind=kLoop, calls=%fused_computation.32 | loop fusion | flops 458752 | bytes 786432 | tf_op jit(solution)/shard_map/reduce_sum | solution.py:61
  62.6 1.7 %reshape.46 = f32[2,2,4,16,16,16]{5,4,3,2,1,0:T(8,128)S(1)} reshape(f32[2,2,64,256]{3,2,1,0:T(8,128)} %convert_reduce_fusion) | data formatting | bytes 524288 | tf_op jit(solution)/shard_map/reshape | solution.py:62
  64.3 2.0 %copy.10 = f32[2,2,4,16,16,16]{5,4,3,2,0,1:T(8,128)} copy(f32[2,2,4,16,16,16]{5,3,4,2,1,0:T(8,128)S(1)} %bitcast.106) | data formatting | bytes 524288 | tf_op jit(solution)/shard_map/transpose | solution.py:62
  66.3 2.6 %reshape.47 = f32[2,2,64,256]{3,2,0,1:T(8,128)S(1)} reshape(f32[2,2,4,16,16,16]{5,4,3,2,0,1:T(8,128)} %copy.10) | data formatting | bytes 524288 | tf_op jit(solution)/shard_map/reshape | solution.py:62
  68.9 0.0 copy-done.2
  68.9 0.0 copy-done.3
  68.9 1.5 %fusion.28 = bf16[2,2,64,256]{3,2,1,0:T(8,128)(2,1)} fusion(f32[2,2,64,256]{3,2,0,1:T(8,128)S(1)} %reshape.47, bf16[2,256,1400,1]{1,2,3,0:T(8,128)(2,1)S(1)} %copy-done.4, bf16[2,2,64,512]{3,2,0,1:T(8,128)(2,1)S(1)} %bitcast.110, bf16[512,1400]{0,1:T(8,128)(2,1)S(1)} %copy-done, f32[1400]{0:T(1024)S(1)} %copy-done.3), kind=kOutput, calls=%fused_computation.29 | convolution fusion | flops 552132608 | bytes 3528160 | tf_op jit(solution)/shard_map/abpg,bqg->abpq/dot_general | solution.py:67
  (8 shorter events, 0.0 us)
Async XLA Ops:
  0.0 40.7 %copy-start = (bf16[512,1400]{0,1:T(8,128)(2,1)S(1)}, bf16[512,1400]{0,1:T(8,128)(2,1)}, u32[]{:S(2)}) copy-start(bf16[512,1400]{0,1:T(8,128)(2,1)} %param.6) | copy-start | bytes 4300804
  0.0 39.9 %collective-permute-start = (bf16[2,32,512]{2,1,0:T(8,128)(2,1)}, bf16[2,32,512]{2,1,0:T(8,128)(2,1)S(1)}, u32[]{:S(2)}, u32[]{:S(2)}) collective-permute-start(bf16[2,32,512]{2,1,0:T(8,128)(2,1)} %param.5), channel_id=1, source_target_pairs={{0,1020},{4,0},{8,4},{12,8},{16,12},{20,16},{24,20},{28,24},{32,28... | collective-permute-start | bytes 196616 | tf_op jit(solution)/shard_map/ppermute | solution.py:14
  24.8 15.1 %collective-permute-start.1 = (bf16[2,32,512]{2,1,0:T(8,128)(2,1)}, bf16[2,32,512]{2,1,0:T(8,128)(2,1)S(1)}, u32[]{:S(2)}, u32[]{:S(2)}) collective-permute-start(bf16[2,32,512]{2,1,0:T(8,128)(2,1)} %param.5), channel_id=1, source_target_pairs={{0,1016},{4,1020},{8,0},{12,4},{16,8},{20,12},{24,16},{28,20},{32,... | collective-permute-start | bytes 196616 | tf_op jit(solution)/shard_map/ppermute | solution.py:14
  40.7 2.1 %copy-start.1 = (bf16[5600,350]{0,1:T(8,128)(2,1)S(1)}, bf16[5600,350]{0,1:T(8,128)(2,1)}, u32[]{:S(2)}) copy-start(bf16[5600,350]{0,1:T(8,128)(2,1)} %reshape.44) | copy-start | bytes 11760004
  49.3 12.5 %all-to-all-start = ((bf16[4,2,2,64,256]{4,3,2,1,0:T(8,128)(2,1)}), bf16[4,2,2,64,256]{4,3,2,1,0:T(8,128)(2,1)S(1)}, u32[]{:S(2)}, u32[]{:S(2)}) async-start(bf16[4,2,2,64,256]{4,3,2,1,0:T(8,128)(2,1)} %bitcast.105), calls=%async_computation | async-start | bytes 1048576 | tf_op jit(solution)/shard_map/all_to_all | solution.py:60
  66.3 2.6 %copy-start.2 = (bf16[2,2,4,16,512]{4,3,2,0,1:T(8,128)(2,1)S(1)}, bf16[2,2,4,16,512]{4,3,2,0,1:T(8,128)(2,1)}, u32[]{:S(2)}) copy-start(bf16[2,2,4,16,512]{4,3,2,0,1:T(8,128)(2,1)} %multiply_convert_fusion) | copy-start | bytes 786436
  66.3 2.6 %copy-start.3 = (f32[1400]{0:T(1024)S(1)}, f32[1400]{0:T(1024)}, u32[]{:S(2)}) copy-start(f32[1400]{0:T(1024)} %param.8) | copy-start | bytes 16804
  66.3 2.6 %copy-start.4 = (bf16[2,256,1400,1]{1,2,3,0:T(8,128)(2,1)S(1)}, bf16[2,256,1400,1]{1,2,3,0:T(8,128)(2,1)}, u32[]{:S(2)}) copy-start(bf16[2,256,1400,1]{1,2,3,0:T(8,128)(2,1)} %fusion) | copy-start | bytes 4300804

commit v2 on v1

--- a/solution.py
+++ b/solution.py
@@ -2,6 +2,8 @@
 import jax.numpy as jnp
 from jax import lax
 from jax.sharding import PartitionSpec as P
+from jax.experimental import pallas as pl
+from jax.experimental.pallas import tpu as pltpu
 
 NV = 16
 NC = 16
@@ -25,6 +27,41 @@
     return jnp.einsum("...pm,mg->...pg", prod, fit, preferred_element_type=jnp.float32).astype(jnp.bfloat16)
 
 
+def nt(left, right):
+    return lax.dot_general(left, right, (((1,), (1,)), ((), ())), preferred_element_type=jnp.float32)
+
+
+def direct_kernel(q_ref, cond_pairs_ref, vale_pairs_ref, fit_ref, fit_part_ref, screen_ref, out_ref):
+    q = q_ref[pl.program_id(0)]
+    cond = nt(cond_pairs_ref[0], fit_ref[...]).astype(jnp.bfloat16)
+    inter = lax.switch(q, [lambda i=i: screen_ref[:, i, :] for i in range(screen_ref.shape[1])])
+    screened = nt(cond, inter).astype(jnp.bfloat16)
+    vale = nt(vale_pairs_ref[0], fit_part_ref[...]).astype(jnp.bfloat16)
+    out_ref[0] = nt(vale, screened).astype(jnp.bfloat16)
+
+
+def direct_terms(q, cond_pairs, vale_pairs, fit_t, fit_part_t, screen_t):
+    blocks, rows, mu = cond_pairs.shape
+    vrows = vale_pairs.shape[1]
+    full = lambda shape: pl.BlockSpec(shape, lambda b, q: (0,) * len(shape))
+    return pl.pallas_call(
+        direct_kernel,
+        out_shape=jax.ShapeDtypeStruct((blocks, vrows, rows), jnp.bfloat16),
+        grid_spec=pltpu.PrefetchScalarGridSpec(
+            num_scalar_prefetch=1,
+            grid=(blocks,),
+            in_specs=[
+                pl.BlockSpec((1, rows, mu), lambda b, q: (b, 0, 0)),
+                pl.BlockSpec((1, vrows, mu), lambda b, q: (b, 0, 0)),
+                full(fit_t.shape),
+                full(fit_part_t.shape),
+                full(screen_t.shape),
+            ],
+            out_specs=pl.BlockSpec((1, vrows, rows), lambda b, q: (b, 0, 0)),
+        ),
+    )(q, cond_pairs, vale_pairs, fit_t, fit_part_t, screen_t)
+
+
 def shards(orbitals, fitting, screen, coulomb, qindex):
     per_dev = orbitals.shape[0]
     npair = lax.axis_size("pair")
@@ -33,28 +70,22 @@
     width = screen.shape[2]
     ng = screen.shape[1]
     vr = NV // npair
-    fitting_part = lax.dynamic_slice_in_dim(fitting, pair_index * width, width, 1)
 
     rows = jnp.stack([from_behind(orbitals, "kloop", -s) for s in range(1, S + 1)], 0)
     cols = jnp.broadcast_to(orbitals[None], rows.shape)
 
     own = fields(orbitals[:, :NV], orbitals[:, NV:], fitting)
 
-    cond = fields(rows[:, :, NV:], cols[:, :, NV:], fitting)
-    vale = fields(rows[:, :, :NV], cols[:, :, :NV], fitting_part)
+    blocks = S * per_dev
+    cond_pairs = products(rows[:, :, NV:], cols[:, :, NV:]).reshape(blocks, NC * NC, -1)
+    vale_pairs = products(rows[:, :, :NV], cols[:, :, :NV]).reshape(blocks, NV * NV, -1)
+    fit_t = fitting.T
+    fit_part_t = lax.dynamic_slice_in_dim(fit_t, pair_index * width, width, 0)
 
-    screen2d = screen.reshape(screen.shape[0] * ng, width)
-    screened = []
-    for s in range(S):
-        row_s = []
-        for lk in range(per_dev):
-            q = qindex[loop_index * per_dev + lk, s]
-            inter = lax.dynamic_slice_in_dim(screen2d, q * ng, ng, 0)
-            row_s.append(jnp.dot(cond[s, lk], inter, preferred_element_type=jnp.float32).astype(jnp.bfloat16))
-        screened.append(jnp.stack(row_s, 0))
-    screened = jnp.stack(screened, 0)
-
-    terms = jnp.einsum("abpg,abqg->abpq", vale, screened, preferred_element_type=jnp.float32).astype(jnp.bfloat16)
+    nq = screen.shape[0]
+    qs = jnp.stack([qindex[loop_index * per_dev + lk, s] for s in range(S) for lk in range(per_dev)])
+    qs = jnp.clip(qs, 0, nq - 1)
+    terms = direct_terms(qs, cond_pairs, vale_pairs, fit_t, fit_part_t, jnp.transpose(screen, (2, 0, 1)))
     terms = terms.reshape(S, per_dev, npair, vr * NV, NC * NC)
     terms = jnp.moveaxis(terms, 2, 0)
     got = lax.all_to_all(terms, "pair", 0, 0, tiled=True)

time: 71 us -> 80.8 us (1.14)
  Pallas kernels: 0 us -> 21.1 us
  matrix products: 9.3 us -> 3.55 us
  local copies, waits for them, and re-layouts: 17 us -> 11.6 us
  other arithmetic: 4.55 us -> 7.44 us
  between operations: 2.72 us -> 0.1 us
    pallas_call x0 -> x1, Pallas kernels: none -> 21.1 us  [direct_terms(): pl.pallas_call(direct_kernel, out_shape=jax.ShapeDtypeStruct((blocks, vro...]
    reshape x1 -> x0, local copies, waits for them, and re-layouts: 7.8 us -> none  [shards(): screen2d = screen.reshape(screen.shape[0] * ng, width)]
    dot_general x5 -> x0, matrix products: 4.07 us -> none  [the longest x4 2.14 us: shards(): jnp.dot(cond[s, lk], inter, preferred_element_type=jnp.float32)]
    min x0 -> x1, other arithmetic: none -> 3.08 us  [shards(): qs = jnp.clip(qs, 0, nq - 1)]
    dynamic_slice x1 -> x2, local copies, waits for them, and re-layouts: 1.49 us -> 3.31 us  [the longest x1 1.83 us: shards(): fit_part_t = lax.dynamic_slice_in_dim(fit_t, pair_index * width, width, 0)]
    dot_general x2 -> x1, matrix products: 3.75 us -> 2.05 us  [fields(): jnp.einsum('...pm,mg->...pg', prod, fit, preferred_element_type=jnp.float32)]
    another operation x2 -> x0, other arithmetic: 1.54 us -> none  [shards(): screened = jnp.stack(screened, 0)]
    convert_element_type x3, other arithmetic: 1.37 us -> 2.75 us  [products(): prod.astype(jnp.bfloat16)]
  transfers between devices with their start and end apart: 3 -> 3, of which waited for: 1 -> 1; matrix products, arithmetic and copies ran while one was open for 18% -> 13% of each run, Pallas kernels for 0% -> 0%
where the time goes in v2:
time: 80.8 us; the launch traced here: 80.4 us
  starting transfers between devices  31.7 us (39%)
  Pallas kernels  21.1 us (26%)
  local copies, waits for them, and re-layouts  11.6 us (14%)
  other arithmetic  7.44 us (9%)
  waiting for transfers between devices  4.96 us (6%)
  matrix products  3.55 us (4%)
    ppermute x2, starting transfers between devices, from_behind(): return lax.ppermute(value, axis, pairs)  27.1 us
    pallas_call x1, Pallas kernels, direct_terms(): pl.pallas_call(direct_kernel, out_shape=jax.ShapeDtypeStruct((blocks, vro...  21.1 us
    all_to_all x1, waiting for transfers between devices, shards(): got = lax.all_to_all(terms, 'pair', 0, 0, tiled=True)  4.95 us
    all_to_all x1, starting transfers between devices, shards(): got = lax.all_to_all(terms, 'pair', 0, 0, tiled=True)  4.67 us
    reshape x2, local copies, waits for them, and re-layouts, shards(): dsum.reshape(S, per_dev, vr, NV, NC, NC).transpose(0, 1, 2, 4, 3, 5)  4.23 us
    min x1, other arithmetic, shards(): qs = jnp.clip(qs, 0, nq - 1)  3.08 us
    convert_element_type x3, other arithmetic, products(): prod.astype(jnp.bfloat16)  2.75 us
    dot_general x1, matrix products, fields(): jnp.einsum('...pm,mg->...pg', prod, fit, preferred_element_type=jnp.float32)  2.05 us
  transfers between devices with their start and end apart: 3, of which 1 were waited for; matrix products, arithmetic and copies ran while one was open for 13% of the time, Pallas kernels for 0%

profile of v2, /device:TPU:1, one launch (start us, length us, event | category | flops | bytes accessed | tf_op | source)
XLA Modules:
  0.0 80.4 jit_solution(6813183074235914578)
XLA Ops:
  0.0 24.6 %collective-permute-start = (bf16[2,32,512]{2,1,0:T(8,128)(2,1)}, bf16[2,32,512]{2,1,0:T(8,128)(2,1)S(1)}, u32[]{:S(2)}, u32[]{:S(2)}) collective-permute-start(bf16[2,32,512]{2,1,0:T(8,128)(2,1)} %param.5), channel_id=1, source_target_pairs={{0,1020},{4,0},{8,4},{12,8},{16,12},{20,16},{24,20},{28,24},{32,28... | collective-permute-start | bytes 196616 | tf_op jit(solution)/shard_map/ppermute | solution.py:16
  24.6 2.4 %collective-permute-start.1 = (bf16[2,32,512]{2,1,0:T(8,128)(2,1)}, bf16[2,32,512]{2,1,0:T(8,128)(2,1)S(1)}, u32[]{:S(2)}, u32[]{:S(2)}) collective-permute-start(bf16[2,32,512]{2,1,0:T(8,128)(2,1)} %param.5), channel_id=1, source_target_pairs={{0,1016},{4,1020},{8,0},{12,4},{16,8},{20,12},{24,16},{28,20},{32,... | collective-permute-start | bytes 196616 | tf_op jit(solution)/shard_map/ppermute | solution.py:16
  27.1 0.8 %slice_convert_fusion.1 = (f32[2,16,512]{2,1,0:T(8,128)S(1)}, f32[2,16,512]{2,1,0:T(8,128)S(1)}) fusion(bf16[2,32,512]{2,1,0:T(8,128)(2,1)} %param.5), kind=kLoop, calls=%fused_computation.31 | loop fusion | flops 32768 | bytes 196608 | tf_op jit(solution)/shard_map/convert_element_type | solution.py:20
  27.9 1.8 %dynamic-slice_bitcast_fusion.fit_part_ref = bf16[350,512]{1,0:T(8,128)(2,1)} fusion(bf16[512,1400]{0,1:T(8,128)(2,1)} %param.6, s32[]{:T(128)S(6)} %select_n.17), kind=kLoop, calls=%fused_computation.21 | loop fusion | bytes 716804 | tf_op jit(solution)/shard_map/dynamic_slice | solution.py:83
  29.7 1.5 %constant_dynamic-slice_fusion.1 = (s32[1,1]{0,1:T(1,128)}, s32[1,1]{0,1:T(1,128)}, s32[1,1]{0,1:T(1,128)}, s32[1,1]{0,1:T(1,128)}) fusion(s32[512,2]{0,1:T(2,128)} %param.9, s32[]{:T(128)S(6)} %select_n.15, s32[]{:T(128)S(6)} %select_n.16), kind=kLoop, calls=%fused_computation.35 | loop fusion | bytes 40 | tf_op jit(solution)/shard_map/dynamic_slice | solution.py:86
  31.2 3.1 %add_clamp_fusion.q_ref = s32[4]{0:T(128)} fusion(s32[1]{0:T(128)} %bitcast.12, s32[1]{0:T(128)} %bitcast.11, s32[1]{0:T(128)} %bitcast.10, s32[1]{0:T(128)} %bitcast.9), kind=kLoop, calls=%fused_computation.36 | loop fusion | flops 16 | bytes 32 | tf_op jit(solution)/shard_map/jit(clip)/min | solution.py:87
  34.3 0.0 collective-permute-done
  34.3 0.0 collective-permute-done.1
  34.3 1.9 %multiply_convert_fusion = (bf16[2,2,16,16,512]{4,3,2,1,0:T(8,128)(2,1)}, bf16[2,2,16,16,512]{4,3,2,1,0:T(8,128)(2,1)}) fusion(f32[2,16,512]{2,1,0:T(8,128)S(1)} %get-tuple-element.7, f32[2,2,16,512]{3,2,1,0:T(8,128)S(1)} %get-tuple-element.5, f32[2,16,512]{2,1,0:T(8,128)S(1)} %get-tuple-element.8, f32[2,2,16,512]{3,2,1,0:T(8,128)S(1)} %get-tuple-element.6), kind=kLoop, calls=%fused_computation.6 | loop fusion | flops 2097152 | bytes 2490368 | tf_op jit(solution)/shard_map/convert_element_type | solution.py:22
  36.2 21.1 %shard_map.55 = bf16[4,256,256]{2,1,0:T(8,128)(2,1)} custom-call(s32[4]{0:T(128)} %add_clamp_fusion.q_ref, bf16[4,256,512]{2,1,0:T(8,128)(2,1)} %bitcast.62, bf16[4,256,512]{2,1,0:T(8,128)(2,1)} %bitcast.61, bf16[1400,512]{1,0:T(8,128)(2,1)} %bitcast.64, bf16[350,512]{1,0:T(8,128)(2,1)} %dynamic-slice_bitcast_fusion.fit_part_ref, bf16[350,4,1400]{2,1,0:T(4,128)(2,1)} %bitcast.63), custom_call_target="tpu_custom_call" | custom-call | tf_op jit(solution)/shard_map/pallas_call | solution.py:47
  57.3 0.0 copy-start
  57.3 2.0 %copy.17 = bf16[2,2,4,64,256]{4,3,1,0,2:T(8,128)(2,1)} copy(bf16[2,2,4,64,256]{4,3,2,1,0:T(8,128)(2,1)} %bitcast.65) | data formatting | bytes 1048576 | tf_op jit(solution)/shard_map/reshape | solution.py:89
  59.3 4.7 %all-to-all-start = ((bf16[4,2,2,64,256]{4,3,2,1,0:T(8,128)(2,1)}), bf16[4,2,2,64,256]{4,3,2,1,0:T(8,128)(2,1)S(1)}, u32[]{:S(2)}, u32[]{:S(2)}) async-start(bf16[4,2,2,64,256]{4,3,2,1,0:T(8,128)(2,1)} %bitcast.59), calls=%async_computation | async-start | bytes 1048576 | tf_op jit(solution)/shard_map/all_to_all | solution.py:91
  64.0 0.1 multiply_convert_fusion.2
  64.1 0.0 copy-done
  64.1 2.0 %fusion = bf16[2,256,1400,1]{1,2,3,0:T(8,128)(2,1)} fusion(bf16[2,256,512]{2,1,0:T(8,128)(2,1)S(1)} %bitcast.66, bf16[512,1400]{0,1:T(8,128)(2,1)S(1)} %copy-done), kind=kOutput, calls=%fused_computation.1 | convolution fusion | flops 734720000 | bytes 3391488 | tf_op jit(solution)/shard_map/...pm,mg->...pg/dot_general | solution.py:27
  66.1 0.7 multiply_convert_fusion.3
  66.9 5.0 %all-to-all-done = bf16[4,2,2,64,256]{4,3,2,1,0:T(8,128)(2,1)S(1)} async-done(((bf16[4,2,2,64,256]{4,3,2,1,0:T(8,128)(2,1)}), bf16[4,2,2,64,256]{4,3,2,1,0:T(8,128)(2,1)S(1)}, u32[]{:S(2)}, u32[]{:S(2)}) %all-to-all-start) | async-done | bytes 524320 | tf_op jit(solution)/shard_map/all_to_all | solution.py:91
  71.8 0.8 convert_reduce_fusion
  72.6 1.7 %reshape.36 = f32[2,2,4,16,16,16]{5,4,3,2,1,0:T(8,128)S(1)} reshape(f32[2,2,64,256]{3,2,1,0:T(8,128)} %convert_reduce_fusion) | data formatting | bytes 524288 | tf_op jit(solution)/shard_map/reshape | solution.py:93
  74.3 2.0 %copy.10 = f32[2,2,4,16,16,16]{5,4,3,2,0,1:T(8,128)} copy(f32[2,2,4,16,16,16]{5,3,4,2,1,0:T(8,128)S(1)} %bitcast.60) | data formatting | bytes 524288 | tf_op jit(solution)/shard_map/transpose | solution.py:93
  76.3 0.0 copy-start.1
  76.3 0.0 copy-start.2
  76.3 0.0 copy-start.3
  76.3 2.6 %reshape.37 = f32[2,2,64,256]{3,2,0,1:T(8,128)S(1)} reshape(f32[2,2,4,16,16,16]{5,4,3,2,0,1:T(8,128)} %copy.10) | data formatting | bytes 524288 | tf_op jit(solution)/shard_map/reshape | solution.py:93
  78.9 0.0 copy-done.1
  78.9 0.0 copy-done.2
  78.9 0.0 copy-done.3
  78.9 1.5 %fusion.21 = bf16[2,2,64,256]{3,2,1,0:T(8,128)(2,1)} fusion(f32[2,2,64,256]{3,2,0,1:T(8,128)S(1)} %reshape.37, bf16[2,256,1400,1]{1,2,3,0:T(8,128)(2,1)S(1)} %copy-done.3, bf16[2,2,64,512]{3,2,0,1:T(8,128)(2,1)S(1)} %bitcast.67, bf16[512,1400]{0,1:T(8,128)(2,1)S(1)} %copy-done, f32[1400]{0:T(1024)S(1)} %copy-done.2), kind=kOutput, calls=%fused_computation.15 | convolution fusion | flops 552132608 | bytes 3528160 | tf_op jit(solution)/shard_map/abpg,bqg->abpq/dot_general | solution.py:98
  (1 shorter events, 0.0 us)
Async XLA Ops:
  0.0 34.3 %collective-permute-start = (bf16[2,32,512]{2,1,0:T(8,128)(2,1)}, bf16[2,32,512]{2,1,0:T(8,128)(2,1)S(1)}, u32[]{:S(2)}, u32[]{:S(2)}) collective-permute-start(bf16[2,32,512]{2,1,0:T(8,128)(2,1)} %param.5), channel_id=1, source_target_pairs={{0,1020},{4,0},{8,4},{12,8},{16,12},{20,16},{24,20},{28,24},{32,28... | collective-permute-start | bytes 196616 | tf_op jit(solution)/shard_map/ppermute | solution.py:16
  24.6 9.7 %collective-permute-start.1 = (bf16[2,32,512]{2,1,0:T(8,128)(2,1)}, bf16[2,32,512]{2,1,0:T(8,128)(2,1)S(1)}, u32[]{:S(2)}, u32[]{:S(2)}) collective-permute-start(bf16[2,32,512]{2,1,0:T(8,128)(2,1)} %param.5), channel_id=1, source_target_pairs={{0,1016},{4,1020},{8,0},{12,4},{16,8},{20,12},{24,16},{28,20},{32,... | collective-permute-start | bytes 196616 | tf_op jit(solution)/shard_map/ppermute | solution.py:16
  57.3 6.8 %copy-start = (bf16[512,1400]{0,1:T(8,128)(2,1)S(1)}, bf16[512,1400]{0,1:T(8,128)(2,1)}, u32[]{:S(2)}) copy-start(bf16[512,1400]{0,1:T(8,128)(2,1)} %param.6) | copy-start | bytes 4300804
  59.3 12.5 %all-to-all-start = ((bf16[4,2,2,64,256]{4,3,2,1,0:T(8,128)(2,1)}), bf16[4,2,2,64,256]{4,3,2,1,0:T(8,128)(2,1)S(1)}, u32[]{:S(2)}, u32[]{:S(2)}) async-start(bf16[4,2,2,64,256]{4,3,2,1,0:T(8,128)(2,1)} %bitcast.59), calls=%async_computation | async-start | bytes 1048576 | tf_op jit(solution)/shard_map/all_to_all | solution.py:91
  76.3 2.6 %copy-start.1 = (bf16[2,2,4,16,512]{4,3,2,0,1:T(8,128)(2,1)S(1)}, bf16[2,2,4,16,512]{4,3,2,0,1:T(8,128)(2,1)}, u32[]{:S(2)}) copy-start(bf16[2,2,4,16,512]{4,3,2,0,1:T(8,128)(2,1)} %multiply_convert_fusion.3) | copy-start | bytes 786436
  76.3 2.6 %copy-start.2 = (f32[1400]{0:T(1024)S(1)}, f32[1400]{0:T(1024)}, u32[]{:S(2)}) copy-start(f32[1400]{0:T(1024)} %param.8) | copy-start | bytes 16804
  76.3 2.6 %copy-start.3 = (bf16[2,256,1400,1]{1,2,3,0:T(8,128)(2,1)S(1)}, bf16[2,256,1400,1]{1,2,3,0:T(8,128)(2,1)}, u32[]{:S(2)}) copy-start(bf16[2,256,1400,1]{1,2,3,0:T(8,128)(2,1)} %fusion) | copy-start | bytes 4300804

commit v3 on v2

--- a/solution.py
+++ b/solution.py
@@ -22,6 +22,13 @@
     return prod.astype(jnp.bfloat16).reshape(*lead, prod.shape[-3] * prod.shape[-2], prod.shape[-1])
 
 
+def products_t(left_bands, right_bands):
+    left_t = jnp.swapaxes(left_bands, -1, -2).astype(jnp.float32)
+    right_t = jnp.swapaxes(right_bands, -1, -2).astype(jnp.float32)
+    prod = (left_t[..., :, None] * right_t[..., None, :]).astype(jnp.bfloat16)
+    return prod.reshape(*prod.shape[:-2], prod.shape[-2] * prod.shape[-1])
+
+
 def fields(left_bands, right_bands, fit):
     prod = products(left_bands, right_bands)
     return jnp.einsum("...pm,mg->...pg", prod, fit, preferred_element_type=jnp.float32).astype(jnp.bfloat16)
@@ -33,16 +40,17 @@
 
 def direct_kernel(q_ref, cond_pairs_ref, vale_pairs_ref, fit_ref, fit_part_ref, screen_ref, out_ref):
     q = q_ref[pl.program_id(0)]
-    cond = nt(cond_pairs_ref[0], fit_ref[...]).astype(jnp.bfloat16)
+    cond_t = jnp.dot(fit_ref[...], cond_pairs_ref[0], preferred_element_type=jnp.float32).astype(jnp.bfloat16)
     inter = lax.switch(q, [lambda i=i: screen_ref[:, i, :] for i in range(screen_ref.shape[1])])
-    screened = nt(cond, inter).astype(jnp.bfloat16)
-    vale = nt(vale_pairs_ref[0], fit_part_ref[...]).astype(jnp.bfloat16)
-    out_ref[0] = nt(vale, screened).astype(jnp.bfloat16)
+    screened_t = jnp.dot(inter, cond_t, preferred_element_type=jnp.float32).astype(jnp.bfloat16)
+    vale_t = jnp.dot(fit_part_ref[...], vale_pairs_ref[0], preferred_element_type=jnp.float32).astype(jnp.bfloat16)
+    terms = lax.dot_general(vale_t, screened_t, (((0,), (0,)), ((), ())), preferred_element_type=jnp.float32)
+    out_ref[0] = terms.astype(jnp.bfloat16)
 
 
 def direct_terms(q, cond_pairs, vale_pairs, fit_t, fit_part_t, screen_t):
-    blocks, rows, mu = cond_pairs.shape
-    vrows = vale_pairs.shape[1]
+    blocks, mu, rows = cond_pairs.shape
+    vrows = vale_pairs.shape[2]
     full = lambda shape: pl.BlockSpec(shape, lambda b, q: (0,) * len(shape))
     return pl.pallas_call(
         direct_kernel,
@@ -51,8 +59,8 @@
             num_scalar_prefetch=1,
             grid=(blocks,),
             in_specs=[
-                pl.BlockSpec((1, rows, mu), lambda b, q: (b, 0, 0)),
-                pl.BlockSpec((1, vrows, mu), lambda b, q: (b, 0, 0)),
+                pl.BlockSpec((1, mu, rows), lambda b, q: (b, 0, 0)),
+                pl.BlockSpec((1, mu, vrows), lambda b, q: (b, 0, 0)),
                 full(fit_t.shape),
                 full(fit_part_t.shape),
                 full(screen_t.shape),
@@ -77,8 +85,8 @@
     own = fields(orbitals[:, :NV], orbitals[:, NV:], fitting)
 
     blocks = S * per_dev
-    cond_pairs = products(rows[:, :, NV:], cols[:, :, NV:]).reshape(blocks, NC * NC, -1)
-    vale_pairs = products(rows[:, :, :NV], cols[:, :, :NV]).reshape(blocks, NV * NV, -1)
+    cond_pairs = products_t(rows[:, :, NV:], cols[:, :, NV:]).reshape(blocks, -1, NC * NC)
+    vale_pairs = products_t(rows[:, :, :NV], cols[:, :, :NV]).reshape(blocks, -1, NV * NV)
     fit_t = fitting.T
     fit_part_t = lax.dynamic_slice_in_dim(fit_t, pair_index * width, width, 0)
 

time: 80.8 us -> 84.7 us (1.048)
  local copies, waits for them, and re-layouts: 11.6 us -> 14.2 us
  Pallas kernels: 21.1 us -> 23.7 us
  other arithmetic: 7.44 us -> 6.02 us
    pallas_call x1, Pallas kernels: 21.1 us -> 23.7 us  [direct_terms(): pl.pallas_call(direct_kernel, out_shape=jax.ShapeDtypeStruct((blocks, vro...]
    convert_element_type x0 -> x3, local copies, waits for them, and re-layouts: none -> 2.64 us  [the longest x2 2.62 us: products_t(): prod = (left_t[..., :, None] * right_t[..., None, :]).astype(jnp.bfloat16)]
    convert_element_type x3 -> x2, other arithmetic: 2.75 us -> 0.83 us  [products(): prod.astype(jnp.bfloat16)]
  transfers between devices with their start and end apart: 3 -> 3, of which waited for: 1 -> 1; matrix products, arithmetic and copies ran while one was open for 13% -> 12% of each run, Pallas kernels for 0% -> 0%
where the time goes in v3:
time: 84.7 us; the launch traced here: 84.3 us
  starting transfers between devices  31.7 us (37%)
  Pallas kernels  23.7 us (28%)
  local copies, waits for them, and re-layouts  14.2 us (17%)
  other arithmetic  6.02 us (7%)
  waiting for transfers between devices  4.96 us (6%)
  matrix products  3.52 us (4%)
    ppermute x2, starting transfers between devices, from_behind(): return lax.ppermute(value, axis, pairs)  27.1 us
    pallas_call x1, Pallas kernels, direct_terms(): pl.pallas_call(direct_kernel, out_shape=jax.ShapeDtypeStruct((blocks, vro...  23.7 us
    all_to_all x1, waiting for transfers between devices, shards(): got = lax.all_to_all(terms, 'pair', 0, 0, tiled=True)  4.95 us
    all_to_all x1, starting transfers between devices, shards(): got = lax.all_to_all(terms, 'pair', 0, 0, tiled=True)  4.67 us
    reshape x2, local copies, waits for them, and re-layouts, shards(): dsum.reshape(S, per_dev, vr, NV, NC, NC).transpose(0, 1, 2, 4, 3, 5)  4.23 us
    min x1, other arithmetic, shards(): qs = jnp.clip(qs, 0, nq - 1)  3.08 us
    convert_element_type x2, local copies, waits for them, and re-layouts, products_t(): prod = (left_t[..., :, None] * right_t[..., None, :]).astype(jnp.bfloat16)  2.62 us
    dot_general x1, matrix products, fields(): jnp.einsum('...pm,mg->...pg', prod, fit, preferred_element_type=jnp.float32)  2.05 us
  transfers between devices with their start and end apart: 3, of which 1 were waited for; matrix products, arithmetic and copies ran while one was open for 12% of the time, Pallas kernels for 0%

profile of v3, /device:TPU:1, one launch (start us, length us, event | category | flops | bytes accessed | tf_op | source)
XLA Modules:
  0.0 84.3 jit_solution(3242341585760096457)
XLA Ops:
  0.0 24.6 %collective-permute-start = (bf16[2,32,512]{2,1,0:T(8,128)(2,1)}, bf16[2,32,512]{2,1,0:T(8,128)(2,1)S(1)}, u32[]{:S(2)}, u32[]{:S(2)}) collective-permute-start(bf16[2,32,512]{2,1,0:T(8,128)(2,1)} %param.5), channel_id=1, source_target_pairs={{0,1020},{4,0},{8,4},{12,8},{16,12},{20,16},{24,20},{28,24},{32,28... | collective-permute-start | bytes 196616 | tf_op jit(solution)/shard_map/ppermute | solution.py:16
  24.6 2.4 %collective-permute-start.1 = (bf16[2,32,512]{2,1,0:T(8,128)(2,1)}, bf16[2,32,512]{2,1,0:T(8,128)(2,1)S(1)}, u32[]{:S(2)}, u32[]{:S(2)}) collective-permute-start(bf16[2,32,512]{2,1,0:T(8,128)(2,1)} %param.5), channel_id=1, source_target_pairs={{0,1016},{4,1020},{8,0},{12,4},{16,8},{20,12},{24,16},{28,20},{32,... | collective-permute-start | bytes 196616 | tf_op jit(solution)/shard_map/ppermute | solution.py:16
  27.1 0.8 slice_convert_fusion.1
  27.9 1.8 %dynamic-slice_bitcast_fusion.fit_part_ref = bf16[350,512]{1,0:T(8,128)(2,1)} fusion(bf16[512,1400]{0,1:T(8,128)(2,1)} %param.6, s32[]{:T(128)S(6)} %select_n.17), kind=kLoop, calls=%fused_computation.21 | loop fusion | bytes 716804 | tf_op jit(solution)/shard_map/dynamic_slice | solution.py:91
  29.8 1.5 %constant_dynamic-slice_fusion.1 = (s32[1,1]{0,1:T(1,128)}, s32[1,1]{0,1:T(1,128)}, s32[1,1]{0,1:T(1,128)}, s32[1,1]{0,1:T(1,128)}) fusion(s32[512,2]{0,1:T(2,128)} %param.9, s32[]{:T(128)S(6)} %select_n.15, s32[]{:T(128)S(6)} %select_n.16), kind=kLoop, calls=%fused_computation.37 | loop fusion | bytes 40 | tf_op jit(solution)/shard_map/dynamic_slice | solution.py:94
  31.3 3.1 %add_clamp_fusion.q_ref = s32[4]{0:T(128)} fusion(s32[1]{0:T(128)} %bitcast.12, s32[1]{0:T(128)} %bitcast.11, s32[1]{0:T(128)} %bitcast.10, s32[1]{0:T(128)} %bitcast.9), kind=kLoop, calls=%fused_computation.38 | loop fusion | flops 16 | bytes 32 | tf_op jit(solution)/shard_map/jit(clip)/min | solution.py:95
  34.3 0.0 collective-permute-done
  34.3 0.0 collective-permute-done.1
  34.4 0.2 multiply_convert_fusion.1
  34.6 1.3 %copy.15.cond_pairs_ref = bf16[4,512,256]{2,1,0:T(8,128)(2,1)} copy(bf16[4,512,256]{1,2,0:T(8,128)(2,1)S(1)} %bitcast.69) | data formatting | bytes 2097152 | tf_op jit(solution)/shard_map/convert_element_type | solution.py:28
  35.9 0.2 multiply_convert_fusion
  36.2 1.3 %copy.16.vale_pairs_ref = bf16[4,512,256]{2,1,0:T(8,128)(2,1)} copy(bf16[4,512,256]{1,2,0:T(8,128)(2,1)S(1)} %bitcast.70) | data formatting | bytes 2097152 | tf_op jit(solution)/shard_map/convert_element_type | solution.py:28
  37.5 23.7 %shard_map.55 = bf16[4,256,256]{2,1,0:T(8,128)(2,1)} custom-call(s32[4]{0:T(128)} %add_clamp_fusion.q_ref, bf16[4,512,256]{2,1,0:T(8,128)(2,1)} %copy.15.cond_pairs_ref, bf16[4,512,256]{2,1,0:T(8,128)(2,1)} %copy.16.vale_pairs_ref, bf16[1400,512]{1,0:T(8,128)(2,1)} %bitcast.72, bf16[350,512]{1,0:T(8,128)(2,1)} %dynamic-slice_bitcast_fusion.fit_part_ref, ...), custom_call_target="tpu_custom_call" | custom-call | tf_op jit(solution)/shard_map/pallas_call | solution.py:55
  61.2 0.0 copy-start
  61.2 2.0 %copy.25 = bf16[2,2,4,64,256]{4,3,1,0,2:T(8,128)(2,1)} copy(bf16[2,2,4,64,256]{4,3,2,1,0:T(8,128)(2,1)} %bitcast.73) | data formatting | bytes 1048576 | tf_op jit(solution)/shard_map/reshape | solution.py:97
  63.2 4.7 %all-to-all-start = ((bf16[4,2,2,64,256]{4,3,2,1,0:T(8,128)(2,1)}), bf16[4,2,2,64,256]{4,3,2,1,0:T(8,128)(2,1)S(1)}, u32[]{:S(2)}, u32[]{:S(2)}) async-start(bf16[4,2,2,64,256]{4,3,2,1,0:T(8,128)(2,1)} %bitcast.67), calls=%async_computation | async-start | bytes 1048576 | tf_op jit(solution)/shard_map/all_to_all | solution.py:99
  67.9 0.1 multiply_convert_fusion.2
  68.0 0.0 copy-done
  68.0 2.0 %fusion = bf16[2,256,1400,1]{1,2,3,0:T(8,128)(2,1)} fusion(bf16[2,256,512]{2,1,0:T(8,128)(2,1)S(1)} %bitcast.74, bf16[512,1400]{0,1:T(8,128)(2,1)S(1)} %copy-done), kind=kOutput, calls=%fused_computation.1 | convolution fusion | flops 734720000 | bytes 3391488 | tf_op jit(solution)/shard_map/...pm,mg->...pg/dot_general | solution.py:34
  70.0 0.7 multiply_convert_fusion.3
  70.8 5.0 %all-to-all-done = bf16[4,2,2,64,256]{4,3,2,1,0:T(8,128)(2,1)S(1)} async-done(((bf16[4,2,2,64,256]{4,3,2,1,0:T(8,128)(2,1)}), bf16[4,2,2,64,256]{4,3,2,1,0:T(8,128)(2,1)S(1)}, u32[]{:S(2)}, u32[]{:S(2)}) %all-to-all-start) | async-done | bytes 524320 | tf_op jit(solution)/shard_map/all_to_all | solution.py:99
  75.7 0.8 convert_reduce_fusion
  76.5 1.7 %reshape.38 = f32[2,2,4,16,16,16]{5,4,3,2,1,0:T(8,128)S(1)} reshape(f32[2,2,64,256]{3,2,1,0:T(8,128)} %convert_reduce_fusion) | data formatting | bytes 524288 | tf_op jit(solution)/shard_map/reshape | solution.py:101
  78.2 2.0 %copy.18 = f32[2,2,4,16,16,16]{5,4,3,2,0,1:T(8,128)} copy(f32[2,2,4,16,16,16]{5,3,4,2,1,0:T(8,128)S(1)} %bitcast.68) | data formatting | bytes 524288 | tf_op jit(solution)/shard_map/transpose | solution.py:101
  80.2 0.0 copy-start.1
  80.2 0.0 copy-start.2
  80.2 0.0 copy-start.3
  80.2 2.6 %reshape.39 = f32[2,2,64,256]{3,2,0,1:T(8,128)S(1)} reshape(f32[2,2,4,16,16,16]{5,4,3,2,0,1:T(8,128)} %copy.18) | data formatting | bytes 524288 | tf_op jit(solution)/shard_map/reshape | solution.py:101
  82.8 0.0 copy-done.1
  82.8 0.0 copy-done.2
  82.8 0.0 copy-done.3
  82.8 1.5 %fusion.21 = bf16[2,2,64,256]{3,2,1,0:T(8,128)(2,1)} fusion(f32[2,2,64,256]{3,2,0,1:T(8,128)S(1)} %reshape.39, bf16[2,256,1400,1]{1,2,3,0:T(8,128)(2,1)S(1)} %copy-done.3, bf16[2,2,64,512]{3,2,0,1:T(8,128)(2,1)S(1)} %bitcast.75, bf16[512,1400]{0,1:T(8,128)(2,1)S(1)} %copy-done, f32[1400]{0:T(1024)S(1)} %copy-done.2), kind=kOutput, calls=%fused_computation.15 | convolution fusion | flops 552132608 | bytes 3528160 | tf_op jit(solution)/shard_map/abpg,bqg->abpq/dot_general | solution.py:106
  (2 shorter events, 0.0 us)
Async XLA Ops:
  0.0 34.3 %collective-permute-start = (bf16[2,32,512]{2,1,0:T(8,128)(2,1)}, bf16[2,32,512]{2,1,0:T(8,128)(2,1)S(1)}, u32[]{:S(2)}, u32[]{:S(2)}) collective-permute-start(bf16[2,32,512]{2,1,0:T(8,128)(2,1)} %param.5), channel_id=1, source_target_pairs={{0,1020},{4,0},{8,4},{12,8},{16,12},{20,16},{24,20},{28,24},{32,28... | collective-permute-start | bytes 196616 | tf_op jit(solution)/shard_map/ppermute | solution.py:16
  24.6 9.7 %collective-permute-start.1 = (bf16[2,32,512]{2,1,0:T(8,128)(2,1)}, bf16[2,32,512]{2,1,0:T(8,128)(2,1)S(1)}, u32[]{:S(2)}, u32[]{:S(2)}) collective-permute-start(bf16[2,32,512]{2,1,0:T(8,128)(2,1)} %param.5), channel_id=1, source_target_pairs={{0,1016},{4,1020},{8,0},{12,4},{16,8},{20,12},{24,16},{28,20},{32,... | collective-permute-start | bytes 196616 | tf_op jit(solution)/shard_map/ppermute | solution.py:16
  61.2 6.8 %copy-start = (bf16[512,1400]{0,1:T(8,128)(2,1)S(1)}, bf16[512,1400]{0,1:T(8,128)(2,1)}, u32[]{:S(2)}) copy-start(bf16[512,1400]{0,1:T(8,128)(2,1)} %param.6) | copy-start | bytes 4300804
  63.2 12.5 %all-to-all-start = ((bf16[4,2,2,64,256]{4,3,2,1,0:T(8,128)(2,1)}), bf16[4,2,2,64,256]{4,3,2,1,0:T(8,128)(2,1)S(1)}, u32[]{:S(2)}, u32[]{:S(2)}) async-start(bf16[4,2,2,64,256]{4,3,2,1,0:T(8,128)(2,1)} %bitcast.67), calls=%async_computation | async-start | bytes 1048576 | tf_op jit(solution)/shard_map/all_to_all | solution.py:99
  80.2 2.6 %copy-start.1 = (bf16[2,2,4,16,512]{4,3,2,0,1:T(8,128)(2,1)S(1)}, bf16[2,2,4,16,512]{4,3,2,0,1:T(8,128)(2,1)}, u32[]{:S(2)}) copy-start(bf16[2,2,4,16,512]{4,3,2,0,1:T(8,128)(2,1)} %multiply_convert_fusion.3) | copy-start | bytes 786436
  80.2 2.6 %copy-start.2 = (f32[1400]{0:T(1024)S(1)}, f32[1400]{0:T(1024)}, u32[]{:S(2)}) copy-start(f32[1400]{0:T(1024)} %param.8) | copy-start | bytes 16804
  80.2 2.6 %copy-start.3 = (bf16[2,256,1400,1]{1,2,3,0:T(8,128)(2,1)S(1)}, bf16[2,256,1400,1]{1,2,3,0:T(8,128)(2,1)}, u32[]{:S(2)}) copy-start(bf16[2,256,1400,1]{1,2,3,0:T(8,128)(2,1)} %fusion) | copy-start | bytes 4300804

commit v4 on v3

--- a/solution.py
+++ b/solution.py
@@ -41,8 +41,12 @@
 def direct_kernel(q_ref, cond_pairs_ref, vale_pairs_ref, fit_ref, fit_part_ref, screen_ref, out_ref):
     q = q_ref[pl.program_id(0)]
     cond_t = jnp.dot(fit_ref[...], cond_pairs_ref[0], preferred_element_type=jnp.float32).astype(jnp.bfloat16)
-    inter = lax.switch(q, [lambda i=i: screen_ref[:, i, :] for i in range(screen_ref.shape[1])])
-    screened_t = jnp.dot(inter, cond_t, preferred_element_type=jnp.float32).astype(jnp.bfloat16)
+    every = jnp.dot(screen_ref[...], cond_t, preferred_element_type=jnp.float32).astype(jnp.bfloat16)
+    width = fit_part_ref.shape[0]
+    row = lax.broadcasted_iota(jnp.int32, (width, screen_ref.shape[0]), 0)
+    col = lax.broadcasted_iota(jnp.int32, (width, screen_ref.shape[0]), 1)
+    pick = jnp.where(col == row * (screen_ref.shape[0] // width) + q, 1.0, 0.0).astype(jnp.bfloat16)
+    screened_t = jnp.dot(pick, every, preferred_element_type=jnp.float32).astype(jnp.bfloat16)
     vale_t = jnp.dot(fit_part_ref[...], vale_pairs_ref[0], preferred_element_type=jnp.float32).astype(jnp.bfloat16)
     terms = lax.dot_general(vale_t, screened_t, (((0,), (0,)), ((), ())), preferred_element_type=jnp.float32)
     out_ref[0] = terms.astype(jnp.bfloat16)
@@ -93,7 +97,7 @@
     nq = screen.shape[0]
     qs = jnp.stack([qindex[loop_index * per_dev + lk, s] for s in range(S) for lk in range(per_dev)])
     qs = jnp.clip(qs, 0, nq - 1)
-    terms = direct_terms(qs, cond_pairs, vale_pairs, fit_t, fit_part_t, jnp.transpose(screen, (2, 0, 1)))
+    terms = direct_terms(qs, cond_pairs, vale_pairs, fit_t, fit_part_t, jnp.transpose(screen, (2, 0, 1)).reshape(width * nq, ng))
     terms = terms.reshape(S, per_dev, npair, vr * NV, NC * NC)
     terms = jnp.moveaxis(terms, 2, 0)
     got = lax.all_to_all(terms, "pair", 0, 0, tiled=True)

time: 84.7 us -> 85.7 us (1.012)
  local copies, waits for them, and re-layouts: 14.2 us -> 20.5 us
  Pallas kernels: 23.7 us -> 18.1 us
    reshape x0 -> x1, local copies, waits for them, and re-layouts: none -> 7.14 us  [shards(): jnp.transpose(screen, (2, 0, 1)).reshape(width * nq, ng)]
    pallas_call x1, Pallas kernels: 23.7 us -> 18.1 us  [direct_terms(): pl.pallas_call(direct_kernel, out_shape=jax.ShapeDtypeStruct((blocks, vro...]
  transfers between devices with their start and end apart: 3 -> 3, of which waited for: 1 -> 1; matrix products, arithmetic and copies ran while one was open for 12% -> 19% of each run, Pallas kernels for 0% -> 0%
where the time goes in v4:
time: 85.7 us; the launch traced here: 85.2 us
  starting transfers between devices  31.7 us (37%)
  local copies, waits for them, and re-layouts  20.5 us (24%)
  Pallas kernels  18.1 us (21%)
  other arithmetic  6.15 us (7%)
  waiting for transfers between devices  4.93 us (6%)
  matrix products  3.53 us (4%)
    ppermute x2, starting transfers between devices, from_behind(): return lax.ppermute(value, axis, pairs)  27.1 us
    pallas_call x1, Pallas kernels, direct_terms(): pl.pallas_call(direct_kernel, out_shape=jax.ShapeDtypeStruct((blocks, vro...  18.1 us
    reshape x1, local copies, waits for them, and re-layouts, shards(): jnp.transpose(screen, (2, 0, 1)).reshape(width * nq, ng)  7.14 us
    all_to_all x1, waiting for transfers between devices, shards(): got = lax.all_to_all(terms, 'pair', 0, 0, tiled=True)  4.93 us
    all_to_all x1, starting transfers between devices, shards(): got = lax.all_to_all(terms, 'pair', 0, 0, tiled=True)  4.67 us
    reshape x2, local copies, waits for them, and re-layouts, shards(): dsum.reshape(S, per_dev, vr, NV, NC, NC).transpose(0, 1, 2, 4, 3, 5)  4.23 us
    min x1, other arithmetic, shards(): qs = jnp.clip(qs, 0, nq - 1)  3.19 us
    convert_element_type x2, local copies, waits for them, and re-layouts, products_t(): prod = (left_t[..., :, None] * right_t[..., None, :]).astype(jnp.bfloat16)  2.63 us
  transfers between devices with their start and end apart: 3, of which 1 were waited for; matrix products, arithmetic and copies ran while one was open for 19% of the time, Pallas kernels for 0%

profile of v4, /device:TPU:1, one launch (start us, length us, event | category | flops | bytes accessed | tf_op | source)
XLA Modules:
  0.0 85.2 jit_solution(18156179415722022615)
XLA Ops:
  0.0 24.6 %collective-permute-start = (bf16[2,32,512]{2,1,0:T(8,128)(2,1)}, bf16[2,32,512]{2,1,0:T(8,128)(2,1)S(1)}, u32[]{:S(2)}, u32[]{:S(2)}) collective-permute-start(bf16[2,32,512]{2,1,0:T(8,128)(2,1)} %param.5), channel_id=1, source_target_pairs={{0,1020},{4,0},{8,4},{12,8},{16,12},{20,16},{24,20},{28,24},{32,28... | collective-permute-start | bytes 196616 | tf_op jit(solution)/shard_map/ppermute | solution.py:16
  24.6 2.4 %collective-permute-start.1 = (bf16[2,32,512]{2,1,0:T(8,128)(2,1)}, bf16[2,32,512]{2,1,0:T(8,128)(2,1)S(1)}, u32[]{:S(2)}, u32[]{:S(2)}) collective-permute-start(bf16[2,32,512]{2,1,0:T(8,128)(2,1)} %param.5), channel_id=1, source_target_pairs={{0,1016},{4,1020},{8,0},{12,4},{16,8},{20,12},{24,16},{28,20},{32,... | collective-permute-start | bytes 196616 | tf_op jit(solution)/shard_map/ppermute | solution.py:16
  27.1 0.8 slice_convert_fusion.1
  27.9 0.0 copy-start.2
  27.9 7.1 %reshape.40.screen_ref = bf16[1400,1400]{1,0:T(8,128)(2,1)} reshape(bf16[350,4,1400]{2,1,0:T(4,128)(2,1)} %bitcast.71) | data formatting | bytes 7840000 | tf_op jit(solution)/shard_map/reshape | solution.py:100
  35.1 1.8 %dynamic-slice_bitcast_fusion.fit_part_ref = bf16[350,512]{1,0:T(8,128)(2,1)} fusion(bf16[512,1400]{0,1:T(8,128)(2,1)} %param.6, s32[]{:T(128)S(6)} %select_n.17), kind=kLoop, calls=%fused_computation.21 | loop fusion | bytes 716804 | tf_op jit(solution)/shard_map/dynamic_slice | solution.py:95
  36.9 0.0 copy-done.2
  36.9 0.7 constant_dynamic-slice_fusion.1
  37.6 3.2 %add_clamp_fusion.q_ref = s32[4]{0:T(128)} fusion(s32[1]{0:T(128)} %bitcast.12, s32[1]{0:T(128)} %bitcast.11, s32[1]{0:T(128)} %bitcast.10, s32[1]{0:T(128)} %bitcast.9), kind=kLoop, calls=%fused_computation.38 | loop fusion | flops 16 | bytes 32 | tf_op jit(solution)/shard_map/jit(clip)/min | solution.py:99
  40.8 0.0 collective-permute-done
  40.8 0.0 collective-permute-done.1
  40.8 0.2 multiply_convert_fusion.1
  41.1 1.3 %copy.15.cond_pairs_ref = bf16[4,512,256]{2,1,0:T(8,128)(2,1)} copy(bf16[4,512,256]{1,2,0:T(8,128)(2,1)S(1)} %bitcast.69) | data formatting | bytes 2097152 | tf_op jit(solution)/shard_map/convert_element_type | solution.py:28
  42.4 0.2 multiply_convert_fusion
  42.7 1.3 %copy.16.vale_pairs_ref = bf16[4,512,256]{2,1,0:T(8,128)(2,1)} copy(bf16[4,512,256]{1,2,0:T(8,128)(2,1)S(1)} %bitcast.70) | data formatting | bytes 2097152 | tf_op jit(solution)/shard_map/convert_element_type | solution.py:28
  44.0 18.1 %shard_map.55 = bf16[4,256,256]{2,1,0:T(8,128)(2,1)} custom-call(s32[4]{0:T(128)} %add_clamp_fusion.q_ref, bf16[4,512,256]{2,1,0:T(8,128)(2,1)} %copy.15.cond_pairs_ref, bf16[4,512,256]{2,1,0:T(8,128)(2,1)} %copy.16.vale_pairs_ref, bf16[1400,512]{1,0:T(8,128)(2,1)} %bitcast.72, bf16[350,512]{1,0:T(8,128)(2,1)} %dynamic-slice_bitcast_fusion.fit_part_ref, ...), custom_call_target="tpu_custom_call" | custom-call | tf_op jit(solution)/shard_map/pallas_call | solution.py:59
  62.1 0.0 copy-start
  62.1 2.0 %copy.25 = bf16[2,2,4,64,256]{4,3,1,0,2:T(8,128)(2,1)} copy(bf16[2,2,4,64,256]{4,3,2,1,0:T(8,128)(2,1)} %bitcast.73) | data formatting | bytes 1048576 | tf_op jit(solution)/shard_map/reshape | solution.py:101
  64.1 4.7 %all-to-all-start = ((bf16[4,2,2,64,256]{4,3,2,1,0:T(8,128)(2,1)}), bf16[4,2,2,64,256]{4,3,2,1,0:T(8,128)(2,1)S(1)}, u32[]{:S(2)}, u32[]{:S(2)}) async-start(bf16[4,2,2,64,256]{4,3,2,1,0:T(8,128)(2,1)} %bitcast.67), calls=%async_computation | async-start | bytes 1048576 | tf_op jit(solution)/shard_map/all_to_all | solution.py:103
  68.8 0.1 multiply_convert_fusion.2
  68.9 0.0 copy-done
  68.9 2.1 %fusion = bf16[2,256,1400,1]{1,2,3,0:T(8,128)(2,1)} fusion(bf16[2,256,512]{2,1,0:T(8,128)(2,1)S(1)} %bitcast.74, bf16[512,1400]{0,1:T(8,128)(2,1)S(1)} %copy-done), kind=kOutput, calls=%fused_computation.1 | convolution fusion | flops 734720000 | bytes 3391488 | tf_op jit(solution)/shard_map/...pm,mg->...pg/dot_general | solution.py:34
  70.9 0.8 multiply_convert_fusion.3
  71.7 4.9 %all-to-all-done = bf16[4,2,2,64,256]{4,3,2,1,0:T(8,128)(2,1)S(1)} async-done(((bf16[4,2,2,64,256]{4,3,2,1,0:T(8,128)(2,1)}), bf16[4,2,2,64,256]{4,3,2,1,0:T(8,128)(2,1)S(1)}, u32[]{:S(2)}, u32[]{:S(2)}) %all-to-all-start) | async-done | bytes 524320 | tf_op jit(solution)/shard_map/all_to_all | solution.py:103
  76.6 0.8 convert_reduce_fusion
  77.4 1.7 %reshape.42 = f32[2,2,4,16,16,16]{5,4,3,2,1,0:T(8,128)S(1)} reshape(f32[2,2,64,256]{3,2,1,0:T(8,128)} %convert_reduce_fusion) | data formatting | bytes 524288 | tf_op jit(solution)/shard_map/reshape | solution.py:105
  79.1 2.0 %copy.18 = f32[2,2,4,16,16,16]{5,4,3,2,0,1:T(8,128)} copy(f32[2,2,4,16,16,16]{5,3,4,2,1,0:T(8,128)S(1)} %bitcast.68) | data formatting | bytes 524288 | tf_op jit(solution)/shard_map/transpose | solution.py:105
  81.1 2.6 %reshape.43 = f32[2,2,64,256]{3,2,0,1:T(8,128)S(1)} reshape(f32[2,2,4,16,16,16]{5,4,3,2,0,1:T(8,128)} %copy.18) | data formatting | bytes 524288 | tf_op jit(solution)/shard_map/reshape | solution.py:105
  83.7 0.0 copy-done.1
  83.7 0.0 copy-done.3
  83.7 0.0 copy-done.4
  83.7 1.5 %fusion.21 = bf16[2,2,64,256]{3,2,1,0:T(8,128)(2,1)} fusion(f32[2,2,64,256]{3,2,0,1:T(8,128)S(1)} %reshape.43, bf16[2,256,1400,1]{1,2,3,0:T(8,128)(2,1)S(1)} %copy-done.4, bf16[2,2,64,512]{3,2,0,1:T(8,128)(2,1)S(1)} %bitcast.75, bf16[512,1400]{0,1:T(8,128)(2,1)S(1)} %copy-done, f32[1400]{0:T(1024)S(1)} %copy-done.3), kind=kOutput, calls=%fused_computation.15 | convolution fusion | flops 552132608 | bytes 3528160 | tf_op jit(solution)/shard_map/abpg,bqg->abpq/dot_general | solution.py:110
  (5 shorter events, 0.1 us)
Async XLA Ops:
  0.0 40.8 %collective-permute-start = (bf16[2,32,512]{2,1,0:T(8,128)(2,1)}, bf16[2,32,512]{2,1,0:T(8,128)(2,1)S(1)}, u32[]{:S(2)}, u32[]{:S(2)}) collective-permute-start(bf16[2,32,512]{2,1,0:T(8,128)(2,1)} %param.5), channel_id=1, source_target_pairs={{0,1020},{4,0},{8,4},{12,8},{16,12},{20,16},{24,20},{28,24},{32,28... | collective-permute-start | bytes 196616 | tf_op jit(solution)/shard_map/ppermute | solution.py:16
  24.6 16.2 %collective-permute-start.1 = (bf16[2,32,512]{2,1,0:T(8,128)(2,1)}, bf16[2,32,512]{2,1,0:T(8,128)(2,1)S(1)}, u32[]{:S(2)}, u32[]{:S(2)}) collective-permute-start(bf16[2,32,512]{2,1,0:T(8,128)(2,1)} %param.5), channel_id=1, source_target_pairs={{0,1016},{4,1020},{8,0},{12,4},{16,8},{20,12},{24,16},{28,20},{32,... | collective-permute-start | bytes 196616 | tf_op jit(solution)/shard_map/ppermute | solution.py:16
  27.9 9.0 %copy-start.2 = (s32[512,2]{0,1:T(2,128)S(1)}, s32[512,2]{0,1:T(2,128)}, u32[]{:S(2)}) copy-start(s32[512,2]{0,1:T(2,128)} %param.9) | copy-start | bytes 12292
  62.1 6.8 %copy-start = (bf16[512,1400]{0,1:T(8,128)(2,1)S(1)}, bf16[512,1400]{0,1:T(8,128)(2,1)}, u32[]{:S(2)}) copy-start(bf16[512,1400]{0,1:T(8,128)(2,1)} %param.6) | copy-start | bytes 4300804
  64.1 12.5 %all-to-all-start = ((bf16[4,2,2,64,256]{4,3,2,1,0:T(8,128)(2,1)}), bf16[4,2,2,64,256]{4,3,2,1,0:T(8,128)(2,1)S(1)}, u32[]{:S(2)}, u32[]{:S(2)}) async-start(bf16[4,2,2,64,256]{4,3,2,1,0:T(8,128)(2,1)} %bitcast.67), calls=%async_computation | async-start | bytes 1048576 | tf_op jit(solution)/shard_map/all_to_all | solution.py:103
  81.1 2.6 %copy-start.1 = (bf16[2,2,4,16,512]{4,3,2,0,1:T(8,128)(2,1)S(1)}, bf16[2,2,4,16,512]{4,3,2,0,1:T(8,128)(2,1)}, u32[]{:S(2)}) copy-start(bf16[2,2,4,16,512]{4,3,2,0,1:T(8,128)(2,1)} %multiply_convert_fusion.3) | copy-start | bytes 786436
  81.1 2.6 %copy-start.3 = (f32[1400]{0:T(1024)S(1)}, f32[1400]{0:T(1024)}, u32[]{:S(2)}) copy-start(f32[1400]{0:T(1024)} %param.8) | copy-start | bytes 16804
  81.1 2.6 %copy-start.4 = (bf16[2,256,1400,1]{1,2,3,0:T(8,128)(2,1)S(1)}, bf16[2,256,1400,1]{1,2,3,0:T(8,128)(2,1)}, u32[]{:S(2)}) copy-start(bf16[2,256,1400,1]{1,2,3,0:T(8,128)(2,1)} %fusion) | copy-start | bytes 4300804

commit v5 on v3

--- a/solution.py
+++ b/solution.py
@@ -41,8 +41,14 @@
 def direct_kernel(q_ref, cond_pairs_ref, vale_pairs_ref, fit_ref, fit_part_ref, screen_ref, out_ref):
     q = q_ref[pl.program_id(0)]
     cond_t = jnp.dot(fit_ref[...], cond_pairs_ref[0], preferred_element_type=jnp.float32).astype(jnp.bfloat16)
-    inter = lax.switch(q, [lambda i=i: screen_ref[:, i, :] for i in range(screen_ref.shape[1])])
-    screened_t = jnp.dot(inter, cond_t, preferred_element_type=jnp.float32).astype(jnp.bfloat16)
+    s_all = screen_ref[...].reshape(screen_ref.shape[0] * screen_ref.shape[1], screen_ref.shape[2])
+    every = jnp.dot(s_all, cond_t, preferred_element_type=jnp.float32).astype(jnp.bfloat16)
+    width = fit_part_ref.shape[0]
+    rows_all = screen_ref.shape[0] * screen_ref.shape[1]
+    row = lax.broadcasted_iota(jnp.int32, (width, rows_all), 0)
+    col = lax.broadcasted_iota(jnp.int32, (width, rows_all), 1)
+    pick = jnp.where(col == row * screen_ref.shape[1] + q, 1.0, 0.0).astype(jnp.bfloat16)
+    screened_t = jnp.dot(pick, every, preferred_element_type=jnp.float32).astype(jnp.bfloat16)
     vale_t = jnp.dot(fit_part_ref[...], vale_pairs_ref[0], preferred_element_type=jnp.float32).astype(jnp.bfloat16)
     terms = lax.dot_general(vale_t, screened_t, (((0,), (0,)), ((), ())), preferred_element_type=jnp.float32)
     out_ref[0] = terms.astype(jnp.bfloat16)

time: 84.7 us -> 79.1 us (0.934)
  Pallas kernels: 23.7 us -> 18.1 us
    pallas_call x1, Pallas kernels: 23.7 us -> 18.1 us  [direct_terms(): pl.pallas_call(direct_kernel, out_shape=jax.ShapeDtypeStruct((blocks, vro...]
  transfers between devices with their start and end apart: 3 -> 3, of which waited for: 1 -> 1; matrix products, arithmetic and copies ran while one was open for 12% -> 13% of each run, Pallas kernels for 0% -> 0%
where the time goes in v5:
time: 79.1 us; the launch traced here: 78.7 us
  starting transfers between devices  31.7 us (40%)
  Pallas kernels  18.1 us (23%)
  local copies, waits for them, and re-layouts  14.2 us (18%)
  other arithmetic  6.02 us (8%)
  waiting for transfers between devices  4.95 us (6%)
  matrix products  3.52 us (4%)
    ppermute x2, starting transfers between devices, from_behind(): return lax.ppermute(value, axis, pairs)  27.1 us
    pallas_call x1, Pallas kernels, direct_terms(): pl.pallas_call(direct_kernel, out_shape=jax.ShapeDtypeStruct((blocks, vro...  18.1 us
    all_to_all x1, waiting for transfers between devices, shards(): got = lax.all_to_all(terms, 'pair', 0, 0, tiled=True)  4.95 us
    all_to_all x1, starting transfers between devices, shards(): got = lax.all_to_all(terms, 'pair', 0, 0, tiled=True)  4.67 us
    reshape x2, local copies, waits for them, and re-layouts, shards(): dsum.reshape(S, per_dev, vr, NV, NC, NC).transpose(0, 1, 2, 4, 3, 5)  4.23 us
    min x1, other arithmetic, shards(): qs = jnp.clip(qs, 0, nq - 1)  3.08 us
    convert_element_type x2, local copies, waits for them, and re-layouts, products_t(): prod = (left_t[..., :, None] * right_t[..., None, :]).astype(jnp.bfloat16)  2.62 us
    dot_general x1, matrix products, fields(): jnp.einsum('...pm,mg->...pg', prod, fit, preferred_element_type=jnp.float32)  2.05 us
  transfers between devices with their start and end apart: 3, of which 1 were waited for; matrix products, arithmetic and copies ran while one was open for 13% of the time, Pallas kernels for 0%

profile of v5, /device:TPU:1, one launch (start us, length us, event | category | flops | bytes accessed | tf_op | source)
XLA Modules:
  0.0 78.7 jit_solution(5694516853563815648)
XLA Ops:
  0.0 24.6 %collective-permute-start = (bf16[2,32,512]{2,1,0:T(8,128)(2,1)}, bf16[2,32,512]{2,1,0:T(8,128)(2,1)S(1)}, u32[]{:S(2)}, u32[]{:S(2)}) collective-permute-start(bf16[2,32,512]{2,1,0:T(8,128)(2,1)} %param.5), channel_id=1, source_target_pairs={{0,1020},{4,0},{8,4},{12,8},{16,12},{20,16},{24,20},{28,24},{32,28... | collective-permute-start | bytes 196616 | tf_op jit(solution)/shard_map/ppermute | solution.py:16
  24.6 2.4 %collective-permute-start.1 = (bf16[2,32,512]{2,1,0:T(8,128)(2,1)}, bf16[2,32,512]{2,1,0:T(8,128)(2,1)S(1)}, u32[]{:S(2)}, u32[]{:S(2)}) collective-permute-start(bf16[2,32,512]{2,1,0:T(8,128)(2,1)} %param.5), channel_id=1, source_target_pairs={{0,1016},{4,1020},{8,0},{12,4},{16,8},{20,12},{24,16},{28,20},{32,... | collective-permute-start | bytes 196616 | tf_op jit(solution)/shard_map/ppermute | solution.py:16
  27.1 0.8 %slice_convert_fusion.1 = (f32[2,16,512]{2,1,0:T(8,128)S(1)}, f32[2,16,512]{2,1,0:T(8,128)S(1)}) fusion(bf16[2,32,512]{2,1,0:T(8,128)(2,1)} %param.5), kind=kLoop, calls=%fused_computation.33 | loop fusion | flops 32768 | bytes 196608 | tf_op jit(solution)/shard_map/convert_element_type | solution.py:20
  27.9 1.8 %dynamic-slice_bitcast_fusion.fit_part_ref = bf16[350,512]{1,0:T(8,128)(2,1)} fusion(bf16[512,1400]{0,1:T(8,128)(2,1)} %param.6, s32[]{:T(128)S(6)} %select_n.17), kind=kLoop, calls=%fused_computation.21 | loop fusion | bytes 716804 | tf_op jit(solution)/shard_map/dynamic_slice | solution.py:97
  29.8 1.5 %constant_dynamic-slice_fusion.1 = (s32[1,1]{0,1:T(1,128)}, s32[1,1]{0,1:T(1,128)}, s32[1,1]{0,1:T(1,128)}, s32[1,1]{0,1:T(1,128)}) fusion(s32[512,2]{0,1:T(2,128)} %param.9, s32[]{:T(128)S(6)} %select_n.15, s32[]{:T(128)S(6)} %select_n.16), kind=kLoop, calls=%fused_computation.37 | loop fusion | bytes 40 | tf_op jit(solution)/shard_map/dynamic_slice | solution.py:100
  31.3 3.1 %add_clamp_fusion.q_ref = s32[4]{0:T(128)} fusion(s32[1]{0:T(128)} %bitcast.12, s32[1]{0:T(128)} %bitcast.11, s32[1]{0:T(128)} %bitcast.10, s32[1]{0:T(128)} %bitcast.9), kind=kLoop, calls=%fused_computation.38 | loop fusion | flops 16 | bytes 32 | tf_op jit(solution)/shard_map/jit(clip)/min | solution.py:101
  34.3 0.0 collective-permute-done
  34.3 0.0 collective-permute-done.1
  34.4 0.2 multiply_convert_fusion.1
  34.6 1.3 %copy.15.cond_pairs_ref = bf16[4,512,256]{2,1,0:T(8,128)(2,1)} copy(bf16[4,512,256]{1,2,0:T(8,128)(2,1)S(1)} %bitcast.69) | data formatting | bytes 2097152 | tf_op jit(solution)/shard_map/convert_element_type | solution.py:28
  35.9 0.2 multiply_convert_fusion
  36.2 1.3 %copy.16.vale_pairs_ref = bf16[4,512,256]{2,1,0:T(8,128)(2,1)} copy(bf16[4,512,256]{1,2,0:T(8,128)(2,1)S(1)} %bitcast.70) | data formatting | bytes 2097152 | tf_op jit(solution)/shard_map/convert_element_type | solution.py:28
  37.5 18.1 %shard_map.55 = bf16[4,256,256]{2,1,0:T(8,128)(2,1)} custom-call(s32[4]{0:T(128)} %add_clamp_fusion.q_ref, bf16[4,512,256]{2,1,0:T(8,128)(2,1)} %copy.15.cond_pairs_ref, bf16[4,512,256]{2,1,0:T(8,128)(2,1)} %copy.16.vale_pairs_ref, bf16[1400,512]{1,0:T(8,128)(2,1)} %bitcast.72, bf16[350,512]{1,0:T(8,128)(2,1)} %dynamic-slice_bitcast_fusion.fit_part_ref, ...), custom_call_target="tpu_custom_call" | custom-call | tf_op jit(solution)/shard_map/pallas_call | solution.py:61
  55.6 0.0 copy-start
  55.6 2.0 %copy.25 = bf16[2,2,4,64,256]{4,3,1,0,2:T(8,128)(2,1)} copy(bf16[2,2,4,64,256]{4,3,2,1,0:T(8,128)(2,1)} %bitcast.73) | data formatting | bytes 1048576 | tf_op jit(solution)/shard_map/reshape | solution.py:103
  57.6 4.7 %all-to-all-start = ((bf16[4,2,2,64,256]{4,3,2,1,0:T(8,128)(2,1)}), bf16[4,2,2,64,256]{4,3,2,1,0:T(8,128)(2,1)S(1)}, u32[]{:S(2)}, u32[]{:S(2)}) async-start(bf16[4,2,2,64,256]{4,3,2,1,0:T(8,128)(2,1)} %bitcast.67), calls=%async_computation | async-start | bytes 1048576 | tf_op jit(solution)/shard_map/all_to_all | solution.py:105
  62.3 0.1 multiply_convert_fusion.2
  62.4 0.0 copy-done
  62.4 2.1 %fusion = bf16[2,256,1400,1]{1,2,3,0:T(8,128)(2,1)} fusion(bf16[2,256,512]{2,1,0:T(8,128)(2,1)S(1)} %bitcast.74, bf16[512,1400]{0,1:T(8,128)(2,1)S(1)} %copy-done), kind=kOutput, calls=%fused_computation.1 | convolution fusion | flops 734720000 | bytes 3391488 | tf_op jit(solution)/shard_map/...pm,mg->...pg/dot_general | solution.py:34
  64.5 0.7 multiply_convert_fusion.3
  65.2 4.9 %all-to-all-done = bf16[4,2,2,64,256]{4,3,2,1,0:T(8,128)(2,1)S(1)} async-done(((bf16[4,2,2,64,256]{4,3,2,1,0:T(8,128)(2,1)}), bf16[4,2,2,64,256]{4,3,2,1,0:T(8,128)(2,1)S(1)}, u32[]{:S(2)}, u32[]{:S(2)}) %all-to-all-start) | async-done | bytes 524320 | tf_op jit(solution)/shard_map/all_to_all | solution.py:105
  70.2 0.8 convert_reduce_fusion
  70.9 1.7 %reshape.38 = f32[2,2,4,16,16,16]{5,4,3,2,1,0:T(8,128)S(1)} reshape(f32[2,2,64,256]{3,2,1,0:T(8,128)} %convert_reduce_fusion) | data formatting | bytes 524288 | tf_op jit(solution)/shard_map/reshape | solution.py:107
  72.6 2.0 %copy.18 = f32[2,2,4,16,16,16]{5,4,3,2,0,1:T(8,128)} copy(f32[2,2,4,16,16,16]{5,3,4,2,1,0:T(8,128)S(1)} %bitcast.68) | data formatting | bytes 524288 | tf_op jit(solution)/shard_map/transpose | solution.py:107
  74.6 0.0 copy-start.1
  74.6 0.0 copy-start.2
  74.6 0.0 copy-start.3
  74.6 2.6 %reshape.39 = f32[2,2,64,256]{3,2,0,1:T(8,128)S(1)} reshape(f32[2,2,4,16,16,16]{5,4,3,2,0,1:T(8,128)} %copy.18) | data formatting | bytes 524288 | tf_op jit(solution)/shard_map/reshape | solution.py:107
  77.2 0.0 copy-done.1
  77.2 0.0 copy-done.2
  77.2 0.0 copy-done.3
  77.2 1.5 %fusion.21 = bf16[2,2,64,256]{3,2,1,0:T(8,128)(2,1)} fusion(f32[2,2,64,256]{3,2,0,1:T(8,128)S(1)} %reshape.39, bf16[2,256,1400,1]{1,2,3,0:T(8,128)(2,1)S(1)} %copy-done.3, bf16[2,2,64,512]{3,2,0,1:T(8,128)(2,1)S(1)} %bitcast.75, bf16[512,1400]{0,1:T(8,128)(2,1)S(1)} %copy-done, f32[1400]{0:T(1024)S(1)} %copy-done.2), kind=kOutput, calls=%fused_computation.15 | convolution fusion | flops 552132608 | bytes 3528160 | tf_op jit(solution)/shard_map/abpg,bqg->abpq/dot_general | solution.py:112
  (2 shorter events, 0.0 us)
Async XLA Ops:
  0.0 34.3 %collective-permute-start = (bf16[2,32,512]{2,1,0:T(8,128)(2,1)}, bf16[2,32,512]{2,1,0:T(8,128)(2,1)S(1)}, u32[]{:S(2)}, u32[]{:S(2)}) collective-permute-start(bf16[2,32,512]{2,1,0:T(8,128)(2,1)} %param.5), channel_id=1, source_target_pairs={{0,1020},{4,0},{8,4},{12,8},{16,12},{20,16},{24,20},{28,24},{32,28... | collective-permute-start | bytes 196616 | tf_op jit(solution)/shard_map/ppermute | solution.py:16
  24.6 9.7 %collective-permute-start.1 = (bf16[2,32,512]{2,1,0:T(8,128)(2,1)}, bf16[2,32,512]{2,1,0:T(8,128)(2,1)S(1)}, u32[]{:S(2)}, u32[]{:S(2)}) collective-permute-start(bf16[2,32,512]{2,1,0:T(8,128)(2,1)} %param.5), channel_id=1, source_target_pairs={{0,1016},{4,1020},{8,0},{12,4},{16,8},{20,12},{24,16},{28,20},{32,... | collective-permute-start | bytes 196616 | tf_op jit(solution)/shard_map/ppermute | solution.py:16
  55.6 6.8 %copy-start = (bf16[512,1400]{0,1:T(8,128)(2,1)S(1)}, bf16[512,1400]{0,1:T(8,128)(2,1)}, u32[]{:S(2)}) copy-start(bf16[512,1400]{0,1:T(8,128)(2,1)} %param.6) | copy-start | bytes 4300804
  57.6 12.5 %all-to-all-start = ((bf16[4,2,2,64,256]{4,3,2,1,0:T(8,128)(2,1)}), bf16[4,2,2,64,256]{4,3,2,1,0:T(8,128)(2,1)S(1)}, u32[]{:S(2)}, u32[]{:S(2)}) async-start(bf16[4,2,2,64,256]{4,3,2,1,0:T(8,128)(2,1)} %bitcast.67), calls=%async_computation | async-start | bytes 1048576 | tf_op jit(solution)/shard_map/all_to_all | solution.py:105
  74.6 2.6 %copy-start.1 = (bf16[2,2,4,16,512]{4,3,2,0,1:T(8,128)(2,1)S(1)}, bf16[2,2,4,16,512]{4,3,2,0,1:T(8,128)(2,1)}, u32[]{:S(2)}) copy-start(bf16[2,2,4,16,512]{4,3,2,0,1:T(8,128)(2,1)} %multiply_convert_fusion.3) | copy-start | bytes 786436
  74.6 2.6 %copy-start.2 = (f32[1400]{0:T(1024)S(1)}, f32[1400]{0:T(1024)}, u32[]{:S(2)}) copy-start(f32[1400]{0:T(1024)} %param.8) | copy-start | bytes 16804
  74.6 2.6 %copy-start.3 = (bf16[2,256,1400,1]{1,2,3,0:T(8,128)(2,1)S(1)}, bf16[2,256,1400,1]{1,2,3,0:T(8,128)(2,1)}, u32[]{:S(2)}) copy-start(bf16[2,256,1400,1]{1,2,3,0:T(8,128)(2,1)} %fusion) | copy-start | bytes 4300804

commit v6 on v1

--- a/solution.py
+++ b/solution.py
@@ -44,11 +44,12 @@
     vale = fields(rows[:, :, :NV], cols[:, :, :NV], fitting_part)
 
     screen2d = screen.reshape(screen.shape[0] * ng, width)
+    qs = lax.dynamic_slice_in_dim(qindex, loop_index * per_dev, per_dev, 0)
     screened = []
     for s in range(S):
         row_s = []
         for lk in range(per_dev):
-            q = qindex[loop_index * per_dev + lk, s]
+            q = qs[lk, s]
             inter = lax.dynamic_slice_in_dim(screen2d, q * ng, ng, 0)
             row_s.append(jnp.dot(cond[s, lk], inter, preferred_element_type=jnp.float32).astype(jnp.bfloat16))
         screened.append(jnp.stack(row_s, 0))

time: 71 us -> 70.9 us (level)
    dynamic_slice x1, local copies, waits for them, and re-layouts: 1.49 us -> 0.75 us  [shards(): qs = lax.dynamic_slice_in_dim(qindex, loop_index * per_dev, per_dev, 0)]
where the time goes in v6:
time: 70.9 us; the launch traced here: 70.3 us
  starting transfers between devices  31.9 us (45%)
  local copies, waits for them, and re-layouts  16.9 us (24%)
  matrix products  9.3 us (13%)
  waiting for transfers between devices  4.96 us (7%)
  other arithmetic  4.54 us (6%)
  between operations  2.72 us (4%)
    ppermute x2, starting transfers between devices, from_behind(): return lax.ppermute(value, axis, pairs)  27.2 us
    reshape x1, local copies, waits for them, and re-layouts, shards(): screen2d = screen.reshape(screen.shape[0] * ng, width)  7.8 us
    all_to_all x1, waiting for transfers between devices, shards(): got = lax.all_to_all(terms, 'pair', 0, 0, tiled=True)  4.96 us
    all_to_all x1, starting transfers between devices, shards(): got = lax.all_to_all(terms, 'pair', 0, 0, tiled=True)  4.67 us
    reshape x2, local copies, waits for them, and re-layouts, shards(): dsum.reshape(S, per_dev, vr, NV, NC, NC).transpose(0, 1, 2, 4, 3, 5)  4.23 us
    dot_general x2, matrix products, fields(): jnp.einsum('...pm,mg->...pg', prod, fit, preferred_element_type=jnp.float32)  3.75 us
    dot_general x4, matrix products, shards(): jnp.dot(cond[s, lk], inter, preferred_element_type=jnp.float32)  2.14 us
    transpose x1, local copies, waits for them, and re-layouts, shards(): dsum.reshape(S, per_dev, vr, NV, NC, NC).transpose(0, 1, 2, 4, 3, 5)  2 us
  transfers between devices with their start and end apart: 3, of which 1 were waited for; matrix products, arithmetic and copies ran while one was open for 18% of the time, Pallas kernels for 0%

profile of v6, /device:TPU:1, one launch (start us, length us, event | category | flops | bytes accessed | tf_op | source)
XLA Modules:
  0.0 70.3 jit_solution(11638555654928566197)
XLA Ops:
  0.0 0.0 copy-start
  0.0 24.8 %collective-permute-start = (bf16[2,32,512]{2,1,0:T(8,128)(2,1)}, bf16[2,32,512]{2,1,0:T(8,128)(2,1)S(1)}, u32[]{:S(2)}, u32[]{:S(2)}) collective-permute-start(bf16[2,32,512]{2,1,0:T(8,128)(2,1)} %param.5), channel_id=1, source_target_pairs={{0,1020},{4,0},{8,4},{12,8},{16,12},{20,16},{24,20},{28,24},{32,28... | collective-permute-start | bytes 196616 | tf_op jit(solution)/shard_map/ppermute | solution.py:14
  24.8 2.4 %collective-permute-start.1 = (bf16[2,32,512]{2,1,0:T(8,128)(2,1)}, bf16[2,32,512]{2,1,0:T(8,128)(2,1)S(1)}, u32[]{:S(2)}, u32[]{:S(2)}) collective-permute-start(bf16[2,32,512]{2,1,0:T(8,128)(2,1)} %param.5), channel_id=1, source_target_pairs={{0,1016},{4,1020},{8,0},{12,4},{16,8},{20,12},{24,16},{28,20},{32,... | collective-permute-start | bytes 196616 | tf_op jit(solution)/shard_map/ppermute | solution.py:14
  27.2 0.8 %slice_convert_fusion = (f32[2,16,512]{2,1,0:T(8,128)S(1)}, f32[2,16,512]{2,1,0:T(8,128)S(1)}) fusion(bf16[2,32,512]{2,1,0:T(8,128)(2,1)} %param.5), kind=kLoop, calls=%fused_computation.59 | loop fusion | flops 32768 | bytes 196608 | tf_op jit(solution)/shard_map/convert_element_type | solution.py:18
  28.0 0.8 %constant_dynamic-slice_fusion = s32[2,2]{0,1:T(2,128)S(1)} fusion(s32[512,2]{0,1:T(2,128)} %param.9, s32[]{:T(128)S(6)} %select_n.23), kind=kLoop, calls=%fused_computation.67 | loop fusion | bytes 36 | tf_op jit(solution)/shard_map/dynamic_slice | solution.py:47
  28.8 0.7 fusion.56
  32.0 7.8 %reshape.44 = bf16[5600,350]{0,1:T(8,128)(2,1)} reshape(bf16[4,1400,350]{1,0,2:T(4,128)(2,1)} %param.7) | data formatting | bytes 7840000 | tf_op jit(solution)/shard_map/reshape | solution.py:46
  39.8 0.0 collective-permute-done
  39.8 0.0 collective-permute-done.1
  39.8 0.1 mul.121
  40.0 0.1 mul.135
  40.1 0.5 fusion.4
  40.7 1.7 %convolution_convert_fusion = bf16[2,2,256,1400]{2,3,1,0:T(8,128)(2,1)S(1)} fusion(bf16[2,2,256,512]{3,2,1,0:T(8,128)(2,1)S(1)} %get-tuple-element.13, bf16[512,1400]{0,1:T(8,128)(2,1)S(1)} %copy-done), kind=kOutput, calls=%fused_computation | convolution fusion | flops 1469440000 | bytes 5349376 | tf_op jit(solution)/shard_map/...pm,mg->...pg/dot_general | solution.py:25
  42.4 0.4 copy-done.1
  42.8 0.5 fusion.24
  43.3 0.5 fusion.25
  43.9 0.5 fusion.26
  44.4 0.5 fusion.27
  44.9 0.8 %maximum_bitcast_fusion = bf16[1,2,256,350]{2,3,1,0:T(8,128)(2,1)} fusion(bf16[1,256,350]{1,2,0:T(8,128)(2,1)S(1)} %fusion.25, bf16[1,256,350]{1,2,0:T(8,128)(2,1)S(1)} %fusion.24), kind=kLoop, calls=%fused_computation.47 | loop fusion | flops 179200 | bytes 716800 | tf_op jit(solution)/shard_map/stack | solution.py:56
  45.7 0.8 %maximum_bitcast_fusion.1 = bf16[1,2,256,350]{2,3,1,0:T(8,128)(2,1)} fusion(bf16[1,256,350]{1,2,0:T(8,128)(2,1)S(1)} %fusion.27, bf16[1,256,350]{1,2,0:T(8,128)(2,1)S(1)} %fusion.26), kind=kLoop, calls=%fused_computation.48 | loop fusion | flops 179200 | bytes 716800 | tf_op jit(solution)/shard_map/stack | solution.py:56
  46.5 1.9 %convolution_convert_fusion.4 = bf16[2,2,256,256]{3,2,1,0:T(8,128)(2,1)S(1)} fusion(bf16[2,2,256,512]{3,2,1,0:T(8,128)(2,1)S(1)} %get-tuple-element.14, bf16[1,2,256,350]{2,3,1,0:T(8,128)(2,1)} %maximum_bitcast_fusion.1, bf16[1,2,256,350]{2,3,1,0:T(8,128)(2,1)} %maximum_bitcast_fusion, bf16[512,1400]{0,1:T(8,128)(2,1)S(1)} %copy-done, s32[]{:T(128)S(6)} %select_n.22), kind=kOutput, calls=%fused_computation.15 | convolution fusion | flops 551481344 | bytes 2650116 | tf_op jit(solution)/shard_map/abpg,abqg->abpq/dot_general | solution.py:58
  48.4 0.8 %copy.19 = bf16[2,2,4,64,256]{4,3,1,0,2:T(8,128)(2,1)} copy(bf16[2,2,4,64,256]{4,3,2,1,0:T(8,128)(2,1)S(1)} %bitcast.109) | data formatting | bytes 1048576 | tf_op jit(solution)/shard_map/reshape | solution.py:59
  49.3 4.7 %all-to-all-start = ((bf16[4,2,2,64,256]{4,3,2,1,0:T(8,128)(2,1)}), bf16[4,2,2,64,256]{4,3,2,1,0:T(8,128)(2,1)S(1)}, u32[]{:S(2)}, u32[]{:S(2)}) async-start(bf16[4,2,2,64,256]{4,3,2,1,0:T(8,128)(2,1)} %bitcast.105), calls=%async_computation | async-start | bytes 1048576 | tf_op jit(solution)/shard_map/all_to_all | solution.py:61
  53.9 0.1 fusion.31
  54.0 2.1 %fusion = bf16[2,256,1400,1]{1,2,3,0:T(8,128)(2,1)} fusion(bf16[2,256,512]{2,1,0:T(8,128)(2,1)S(1)} %fusion.31, bf16[512,1400]{0,1:T(8,128)(2,1)S(1)} %copy-done), kind=kOutput, calls=%fused_computation.2 | convolution fusion | flops 734720000 | bytes 3391488 | tf_op jit(solution)/shard_map/...pm,mg->...pg/dot_general | solution.py:25
  56.1 0.8 %multiply_convert_fusion = bf16[2,2,4,16,512]{4,3,2,0,1:T(8,128)(2,1)} fusion(s32[]{:T(128)S(6)} %select_n.21, bf16[1,2,32,512]{3,2,1,0:T(8,128)(2,1)S(1)} %bitcast.114, bf16[1,2,32,512]{3,2,1,0:T(8,128)(2,1)S(1)} %bitcast.112, f32[2,2,16,512]{3,2,1,0:T(8,128)S(1)} %get-tuple-element.5), kind=kLoop, calls=%fused_computation.46 | loop fusion | flops 294912 | bytes 524292 | tf_op jit(solution)/shard_map/convert_element_type | solution.py:20
  56.8 5.0 %all-to-all-done = bf16[4,2,2,64,256]{4,3,2,1,0:T(8,128)(2,1)S(1)} async-done(((bf16[4,2,2,64,256]{4,3,2,1,0:T(8,128)(2,1)}), bf16[4,2,2,64,256]{4,3,2,1,0:T(8,128)(2,1)S(1)}, u32[]{:S(2)}, u32[]{:S(2)}) %all-to-all-start) | async-done | bytes 524320 | tf_op jit(solution)/shard_map/all_to_all | solution.py:61
  61.8 0.8 %convert_reduce_fusion = f32[2,2,64,256]{3,2,1,0:T(8,128)} fusion(bf16[4,2,2,64,256]{4,3,2,1,0:T(8,128)(2,1)S(1)} %all-to-all-done), kind=kLoop, calls=%fused_computation.32 | loop fusion | flops 458752 | bytes 786432 | tf_op jit(solution)/shard_map/reduce_sum | solution.py:62
  62.6 1.7 %reshape.46 = f32[2,2,4,16,16,16]{5,4,3,2,1,0:T(8,128)S(1)} reshape(f32[2,2,64,256]{3,2,1,0:T(8,128)} %convert_reduce_fusion) | data formatting | bytes 524288 | tf_op jit(solution)/shard_map/reshape | solution.py:63
  64.2 2.0 %copy.10 = f32[2,2,4,16,16,16]{5,4,3,2,0,1:T(8,128)} copy(f32[2,2,4,16,16,16]{5,3,4,2,1,0:T(8,128)S(1)} %bitcast.106) | data formatting | bytes 524288 | tf_op jit(solution)/shard_map/transpose | solution.py:63
  66.3 2.6 %reshape.47 = f32[2,2,64,256]{3,2,0,1:T(8,128)S(1)} reshape(f32[2,2,4,16,16,16]{5,4,3,2,0,1:T(8,128)} %copy.10) | data formatting | bytes 524288 | tf_op jit(solution)/shard_map/reshape | solution.py:63
  68.9 1.5 %fusion.28 = bf16[2,2,64,256]{3,2,1,0:T(8,128)(2,1)} fusion(f32[2,2,64,256]{3,2,0,1:T(8,128)S(1)} %reshape.47, bf16[2,256,1400,1]{1,2,3,0:T(8,128)(2,1)S(1)} %copy-done.4, bf16[2,2,64,512]{3,2,0,1:T(8,128)(2,1)S(1)} %bitcast.110, bf16[512,1400]{0,1:T(8,128)(2,1)S(1)} %copy-done, f32[1400]{0:T(1024)S(1)} %copy-done.3), kind=kOutput, calls=%fused_computation.29 | convolution fusion | flops 552132608 | bytes 3528160 | tf_op jit(solution)/shard_map/abpg,bqg->abpq/dot_general | solution.py:68
  (9 shorter events, 0.0 us)
Async XLA Ops:
  0.0 40.6 %copy-start = (bf16[512,1400]{0,1:T(8,128)(2,1)S(1)}, bf16[512,1400]{0,1:T(8,128)(2,1)}, u32[]{:S(2)}) copy-start(bf16[512,1400]{0,1:T(8,128)(2,1)} %param.6) | copy-start | bytes 4300804
  0.0 39.8 %collective-permute-start = (bf16[2,32,512]{2,1,0:T(8,128)(2,1)}, bf16[2,32,512]{2,1,0:T(8,128)(2,1)S(1)}, u32[]{:S(2)}, u32[]{:S(2)}) collective-permute-start(bf16[2,32,512]{2,1,0:T(8,128)(2,1)} %param.5), channel_id=1, source_target_pairs={{0,1020},{4,0},{8,4},{12,8},{16,12},{20,16},{24,20},{28,24},{32,28... | collective-permute-start | bytes 196616 | tf_op jit(solution)/shard_map/ppermute | solution.py:14
  24.8 15.0 %collective-permute-start.1 = (bf16[2,32,512]{2,1,0:T(8,128)(2,1)}, bf16[2,32,512]{2,1,0:T(8,128)(2,1)S(1)}, u32[]{:S(2)}, u32[]{:S(2)}) collective-permute-start(bf16[2,32,512]{2,1,0:T(8,128)(2,1)} %param.5), channel_id=1, source_target_pairs={{0,1016},{4,1020},{8,0},{12,4},{16,8},{20,12},{24,16},{28,20},{32,... | collective-permute-start | bytes 196616 | tf_op jit(solution)/shard_map/ppermute | solution.py:14
  40.7 2.1 %copy-start.1 = (bf16[5600,350]{0,1:T(8,128)(2,1)S(1)}, bf16[5600,350]{0,1:T(8,128)(2,1)}, u32[]{:S(2)}) copy-start(bf16[5600,350]{0,1:T(8,128)(2,1)} %reshape.44) | copy-start | bytes 11760004
  49.3 12.5 %all-to-all-start = ((bf16[4,2,2,64,256]{4,3,2,1,0:T(8,128)(2,1)}), bf16[4,2,2,64,256]{4,3,2,1,0:T(8,128)(2,1)S(1)}, u32[]{:S(2)}, u32[]{:S(2)}) async-start(bf16[4,2,2,64,256]{4,3,2,1,0:T(8,128)(2,1)} %bitcast.105), calls=%async_computation | async-start | bytes 1048576 | tf_op jit(solution)/shard_map/all_to_all | solution.py:61
  66.2 2.6 %copy-start.2 = (bf16[2,2,4,16,512]{4,3,2,0,1:T(8,128)(2,1)S(1)}, bf16[2,2,4,16,512]{4,3,2,0,1:T(8,128)(2,1)}, u32[]{:S(2)}) copy-start(bf16[2,2,4,16,512]{4,3,2,0,1:T(8,128)(2,1)} %multiply_convert_fusion) | copy-start | bytes 786436
  66.2 2.6 %copy-start.3 = (f32[1400]{0:T(1024)S(1)}, f32[1400]{0:T(1024)}, u32[]{:S(2)}) copy-start(f32[1400]{0:T(1024)} %param.8) | copy-start | bytes 16804
  66.3 2.6 %copy-start.4 = (bf16[2,256,1400,1]{1,2,3,0:T(8,128)(2,1)S(1)}, bf16[2,256,1400,1]{1,2,3,0:T(8,128)(2,1)}, u32[]{:S(2)}) copy-start(bf16[2,256,1400,1]{1,2,3,0:T(8,128)(2,1)} %fusion) | copy-start | bytes 4300804

commit v7 on v6

--- a/solution.py
+++ b/solution.py
@@ -66,6 +66,7 @@
     rowf = fields(row_chosen, rows[:, :, NV:], fitting)
     weighted = (rowf.astype(jnp.float32) * coulomb).astype(jnp.bfloat16)
     exchange = jnp.einsum("abpg,bqg->abpq", weighted, own, preferred_element_type=jnp.float32)
+    exchange = lax.optimization_barrier(exchange)
     out = (2.0 * exchange - direct).astype(jnp.bfloat16)
     return jnp.swapaxes(out, 0, 1)
 

time: 70.9 us -> 72.1 us (1.017)
  waiting for transfers between devices: 4.96 us -> 2.85 us
  matrix products: 9.3 us -> 11.4 us
  local copies, waits for them, and re-layouts: 16.9 us -> 18.3 us
  other arithmetic: 4.54 us -> 3.77 us
    all_to_all x1, waiting for transfers between devices: 4.96 us -> 2.84 us  [shards(): got = lax.all_to_all(terms, 'pair', 0, 0, tiled=True)]
    dot_general x1, matrix products: 1.47 us -> 2.87 us  [shards(): jnp.einsum('abpg,bqg->abpq', weighted, own, preferred_element_type=jnp.fl...]
    reshape x1, local copies, waits for them, and re-layouts: 0.83 us -> 1.87 us  [shards(): terms = terms.reshape(S, per_dev, npair, vr * NV, NC * NC)]
    another operation x2, other arithmetic: 1.54 us -> 0.79 us  [shards(): screened = jnp.stack(screened, 0)]
  transfers between devices with their start and end apart: 3 -> 3, of which waited for: 1 -> 1; matrix products, arithmetic and copies ran while one was open for 18% -> 21% of each run, Pallas kernels for 0% -> 0%
where the time goes in v7:
time: 72.1 us; the launch traced here: 71.4 us
  starting transfers between devices  32.5 us (45%)
  local copies, waits for them, and re-layouts  18.3 us (25%)
  matrix products  11.4 us (16%)
  other arithmetic  3.77 us (5%)
  waiting for transfers between devices  2.85 us (4%)
  between operations  2.68 us (4%)
    ppermute x2, starting transfers between devices, from_behind(): return lax.ppermute(value, axis, pairs)  27.8 us
    reshape x1, local copies, waits for them, and re-layouts, shards(): screen2d = screen.reshape(screen.shape[0] * ng, width)  7.81 us
    all_to_all x1, starting transfers between devices, shards(): got = lax.all_to_all(terms, 'pair', 0, 0, tiled=True)  4.67 us
    reshape x2, local copies, waits for them, and re-layouts, shards(): dsum.reshape(S, per_dev, vr, NV, NC, NC).transpose(0, 1, 2, 4, 3, 5)  4.15 us
    dot_general x2, matrix products, fields(): jnp.einsum('...pm,mg->...pg', prod, fit, preferred_element_type=jnp.float32)  3.75 us
    dot_general x1, matrix products, shards(): jnp.einsum('abpg,bqg->abpq', weighted, own, preferred_element_type=jnp.fl...  2.87 us
    all_to_all x1, waiting for transfers between devices, shards(): got = lax.all_to_all(terms, 'pair', 0, 0, tiled=True)  2.84 us
    dot_general x1, matrix products, shards(): jnp.einsum('abpg,abqg->abpq', vale, screened, preferred_element_type=jnp....  2.64 us
  transfers between devices with their start and end apart: 3, of which 1 were waited for; matrix products, arithmetic and copies ran while one was open for 21% of the time, Pallas kernels for 0%

profile of v7, /device:TPU:1, one launch (start us, length us, event | category | flops | bytes accessed | tf_op | source)
XLA Modules:
  0.0 71.4 jit_solution(15959788828380131677)
XLA Ops:
  0.0 25.0 %collective-permute-start.1 = (bf16[2,32,512]{2,1,0:T(8,128)(2,1)}, bf16[2,32,512]{2,1,0:T(8,128)(2,1)S(1)}, u32[]{:S(2)}, u32[]{:S(2)}) collective-permute-start(bf16[2,32,512]{2,1,0:T(8,128)(2,1)} %param.5), channel_id=1, source_target_pairs={{0,1016},{4,1020},{8,0},{12,4},{16,8},{20,12},{24,16},{28,20},{32,... | collective-permute-start | bytes 196616 | tf_op jit(solution)/shard_map/ppermute | solution.py:14
  25.0 2.8 %collective-permute-start = (bf16[2,32,512]{2,1,0:T(8,128)(2,1)}, bf16[2,32,512]{2,1,0:T(8,128)(2,1)S(1)}, u32[]{:S(2)}, u32[]{:S(2)}) collective-permute-start(bf16[2,32,512]{2,1,0:T(8,128)(2,1)} %param.5), channel_id=1, source_target_pairs={{0,1020},{4,0},{8,4},{12,8},{16,12},{20,16},{24,20},{28,24},{32,28... | collective-permute-start | bytes 196616 | tf_op jit(solution)/shard_map/ppermute | solution.py:14
  27.8 0.8 %slice_convert_fusion = (f32[2,16,512]{2,1,0:T(8,128)S(1)}, f32[2,16,512]{2,1,0:T(8,128)S(1)}) fusion(bf16[2,32,512]{2,1,0:T(8,128)(2,1)} %param.5), kind=kLoop, calls=%fused_computation.57 | loop fusion | flops 32768 | bytes 196608 | tf_op jit(solution)/shard_map/convert_element_type | solution.py:18
  28.6 0.8 %constant_dynamic-slice_fusion = s32[2,2]{0,1:T(2,128)S(1)} fusion(s32[512,2]{0,1:T(2,128)} %param.9, s32[]{:T(128)S(6)} %select_n.23), kind=kLoop, calls=%fused_computation.65 | loop fusion | bytes 36 | tf_op jit(solution)/shard_map/dynamic_slice | solution.py:47
  29.4 0.7 fusion.45
  32.5 7.8 %reshape.44 = bf16[5600,350]{0,1:T(8,128)(2,1)} reshape(bf16[4,1400,350]{1,0,2:T(4,128)(2,1)} %param.7) | data formatting | bytes 7840000 | tf_op jit(solution)/shard_map/reshape | solution.py:46
  40.3 0.1 fusion.19
  40.4 0.0 copy-start.3
  40.5 0.1 mul.131
  40.6 0.1 mul.118
  40.7 0.3 copy-done.3
  41.1 0.0 copy-done.5
  41.1 0.5 fusion.4
  41.7 1.7 %convolution_convert_fusion = bf16[2,2,256,1400]{2,3,1,0:T(8,128)(2,1)S(1)} fusion(bf16[2,2,256,512]{3,2,1,0:T(8,128)(2,1)S(1)} %get-tuple-element.13, bf16[512,1400]{0,1:T(8,128)(2,1)S(1)} %copy-done), kind=kOutput, calls=%fused_computation | convolution fusion | flops 1469440000 | bytes 5349376 | tf_op jit(solution)/shard_map/...pm,mg->...pg/dot_general | solution.py:25
  43.4 0.4 copy-done.1
  43.8 0.5 fusion.18
  44.3 0.5 fusion.17
  44.9 0.5 fusion.16
  45.4 0.5 fusion.15
  46.0 0.8 %maximum_bitcast_fusion = bf16[1,2,256,350]{2,3,1,0:T(8,128)(2,1)} fusion(bf16[1,256,350]{1,2,0:T(8,128)(2,1)S(1)} %fusion.16, bf16[1,256,350]{1,2,0:T(8,128)(2,1)S(1)} %fusion.15), kind=kLoop, calls=%fused_computation.43 | loop fusion | flops 179200 | bytes 716800 | tf_op jit(solution)/shard_map/stack | solution.py:56
  46.8 2.6 %convolution_convert_fusion.4 = bf16[2,2,256,256]{3,2,1,0:T(8,128)(2,1)} fusion(bf16[2,2,256,512]{3,2,1,0:T(8,128)(2,1)S(1)} %get-tuple-element.14, bf16[1,2,256,350]{2,3,1,0:T(8,128)(2,1)S(1)} %maximum_bitcast_fusion.1, bf16[1,2,256,350]{2,3,1,0:T(8,128)(2,1)} %maximum_bitcast_fusion, bf16[512,1400]{0,1:T(8,128)(2,1)S(1)} %copy-done, s32[]{:T(128)S(6)} %select_n.22), kind=kOutput, calls=%fused_computation.15 | convolution fusion | flops 551481344 | bytes 2652164 | tf_op jit(solution)/shard_map/abpg,abqg->abpq/dot_general | solution.py:58
  49.4 1.9 %copy.19 = bf16[2,2,4,64,256]{4,3,1,0,2:T(8,128)(2,1)} copy(bf16[2,2,4,64,256]{4,3,2,1,0:T(8,128)(2,1)} %bitcast.95) | data formatting | bytes 1048576 | tf_op jit(solution)/shard_map/reshape | solution.py:59
  51.3 4.7 %all-to-all-start = ((bf16[4,2,2,64,256]{4,3,2,1,0:T(8,128)(2,1)}), bf16[4,2,2,64,256]{4,3,2,1,0:T(8,128)(2,1)S(1)}, u32[]{:S(2)}, u32[]{:S(2)}) async-start(bf16[4,2,2,64,256]{4,3,2,1,0:T(8,128)(2,1)} %bitcast.91), calls=%async_computation | async-start | bytes 1048576 | tf_op jit(solution)/shard_map/all_to_all | solution.py:61
  55.9 2.1 %fusion = bf16[2,256,1400,1]{1,2,3,0:T(8,128)(2,1)} fusion(bf16[2,256,512]{2,1,0:T(8,128)(2,1)S(1)} %fusion.19, bf16[512,1400]{0,1:T(8,128)(2,1)S(1)} %copy-done), kind=kOutput, calls=%fused_computation.2 | convolution fusion | flops 734720000 | bytes 3391488 | tf_op jit(solution)/shard_map/...pm,mg->...pg/dot_general | solution.py:25
  58.0 0.1 multiply_convert_fusion
  58.1 2.9 %fusion.12 = f32[2,2,64,256]{3,2,0,1:T(8,128)} fusion(bf16[2,256,1400,1]{1,2,3,0:T(8,128)(2,1)} %fusion, bf16[2,2,64,512]{3,2,0,1:T(8,128)(2,1)S(1)} %bitcast.96, bf16[512,1400]{0,1:T(8,128)(2,1)S(1)} %copy-done, f32[1400]{0:T(1024)S(1)} %copy-done.7), kind=kOutput, calls=%fused_computation.21 | convolution fusion | flops 551936000 | bytes 3397088 | tf_op jit(solution)/shard_map/abpg,bqg->abpq/dot_general | solution.py:68
  61.0 2.8 %all-to-all-done = bf16[4,2,2,64,256]{4,3,2,1,0:T(8,128)(2,1)S(1)} async-done(((bf16[4,2,2,64,256]{4,3,2,1,0:T(8,128)(2,1)}), bf16[4,2,2,64,256]{4,3,2,1,0:T(8,128)(2,1)S(1)}, u32[]{:S(2)}, u32[]{:S(2)}) %all-to-all-start) | async-done | bytes 524320 | tf_op jit(solution)/shard_map/all_to_all | solution.py:61
  63.8 0.8 %convert_reduce_fusion = f32[2,2,64,256]{3,2,1,0:T(8,128)} fusion(bf16[4,2,2,64,256]{4,3,2,1,0:T(8,128)(2,1)S(1)} %all-to-all-done), kind=kLoop, calls=%fused_computation.28 | loop fusion | flops 458752 | bytes 786432 | tf_op jit(solution)/shard_map/reduce_sum | solution.py:62
  64.6 1.7 %reshape.46 = f32[2,2,4,16,16,16]{5,4,3,2,1,0:T(8,128)S(1)} reshape(f32[2,2,64,256]{3,2,1,0:T(8,128)} %convert_reduce_fusion) | data formatting | bytes 524288 | tf_op jit(solution)/shard_map/reshape | solution.py:63
  66.2 2.0 %copy.10 = f32[2,2,4,16,16,16]{5,4,3,2,0,1:T(8,128)} copy(f32[2,2,4,16,16,16]{5,3,4,2,1,0:T(8,128)S(1)} %bitcast.92) | data formatting | bytes 524288 | tf_op jit(solution)/shard_map/transpose | solution.py:63
  68.2 2.5 %reshape.47 = f32[2,2,64,256]{3,2,0,1:T(8,128)S(1)} reshape(f32[2,2,4,16,16,16]{5,4,3,2,0,1:T(8,128)} %copy.10) | data formatting | bytes 524288 | tf_op jit(solution)/shard_map/reshape | solution.py:63
  70.7 0.7 fusion.32
  (16 shorter events, 0.1 us)
Async XLA Ops:
  0.0 41.6 %copy-start = (bf16[512,1400]{0,1:T(8,128)(2,1)S(1)}, bf16[512,1400]{0,1:T(8,128)(2,1)}, u32[]{:S(2)}) copy-start(bf16[512,1400]{0,1:T(8,128)(2,1)} %param.6) | copy-start | bytes 4300804
  0.0 40.4 %collective-permute-start.1 = (bf16[2,32,512]{2,1,0:T(8,128)(2,1)}, bf16[2,32,512]{2,1,0:T(8,128)(2,1)S(1)}, u32[]{:S(2)}, u32[]{:S(2)}) collective-permute-start(bf16[2,32,512]{2,1,0:T(8,128)(2,1)} %param.5), channel_id=1, source_target_pairs={{0,1016},{4,1020},{8,0},{12,4},{16,8},{20,12},{24,16},{28,20},{32,... | collective-permute-start | bytes 196616 | tf_op jit(solution)/shard_map/ppermute | solution.py:14
  25.0 15.4 %collective-permute-start = (bf16[2,32,512]{2,1,0:T(8,128)(2,1)}, bf16[2,32,512]{2,1,0:T(8,128)(2,1)S(1)}, u32[]{:S(2)}, u32[]{:S(2)}) collective-permute-start(bf16[2,32,512]{2,1,0:T(8,128)(2,1)} %param.5), channel_id=1, source_target_pairs={{0,1020},{4,0},{8,4},{12,8},{16,12},{20,16},{24,20},{28,24},{32,28... | collective-permute-start | bytes 196616 | tf_op jit(solution)/shard_map/ppermute | solution.py:14
  40.4 0.6 copy-start.3
  40.5 0.6 copy-start.5
  41.6 2.1 %copy-start.1 = (bf16[5600,350]{0,1:T(8,128)(2,1)S(1)}, bf16[5600,350]{0,1:T(8,128)(2,1)}, u32[]{:S(2)}) copy-start(bf16[5600,350]{0,1:T(8,128)(2,1)} %reshape.44) | copy-start | bytes 11760004
  51.3 12.5 %all-to-all-start = ((bf16[4,2,2,64,256]{4,3,2,1,0:T(8,128)(2,1)}), bf16[4,2,2,64,256]{4,3,2,1,0:T(8,128)(2,1)S(1)}, u32[]{:S(2)}, u32[]{:S(2)}) async-start(bf16[4,2,2,64,256]{4,3,2,1,0:T(8,128)(2,1)} %bitcast.91), calls=%async_computation | async-start | bytes 1048576 | tf_op jit(solution)/shard_map/all_to_all | solution.py:61
  55.9 2.1 %copy-start.4 = (bf16[2,32,512]{2,1,0:T(8,128)(2,1)S(1)}, bf16[2,32,512]{2,1,0:T(8,128)(2,1)}, u32[]{:S(2)}) copy-start(bf16[2,32,512]{2,1,0:T(8,128)(2,1)} %copy-done.3) | copy-start | bytes 196612
  55.9 2.1 %copy-start.6 = (bf16[2,32,512]{2,1,0:T(8,128)(2,1)S(1)}, bf16[2,32,512]{2,1,0:T(8,128)(2,1)}, u32[]{:S(2)}) copy-start(bf16[2,32,512]{2,1,0:T(8,128)(2,1)} %copy-done.5) | copy-start | bytes 196612
  55.9 2.1 %copy-start.7 = (f32[1400]{0:T(1024)S(1)}, f32[1400]{0:T(1024)}, u32[]{:S(2)}) copy-start(f32[1400]{0:T(1024)} %param.8) | copy-start | bytes 16804
  68.2 2.5 %copy-start.2 = (f32[2,2,64,256]{3,2,0,1:T(8,128)S(1)}, f32[2,2,64,256]{3,2,0,1:T(8,128)}, u32[]{:S(2)}) copy-start(f32[2,2,64,256]{3,2,0,1:T(8,128)} %fusion.12) | copy-start | bytes 786436

commit v8 on v1

--- a/solution.py
+++ b/solution.py
@@ -59,13 +59,14 @@
     terms = jnp.moveaxis(terms, 2, 0)
     got = lax.all_to_all(terms, "pair", 0, 0, tiled=True)
     dsum = jnp.sum(got.astype(jnp.float32), axis=0)
-    direct = dsum.reshape(S, per_dev, vr, NV, NC, NC).transpose(0, 1, 2, 4, 3, 5).reshape(S, per_dev, vr * NC, NV * NC)
 
     row_chosen = lax.dynamic_slice_in_dim(rows, pair_index * vr, vr, 2)
     rowf = fields(row_chosen, rows[:, :, NV:], fitting)
     weighted = (rowf.astype(jnp.float32) * coulomb).astype(jnp.bfloat16)
     exchange = jnp.einsum("abpg,bqg->abpq", weighted, own, preferred_element_type=jnp.float32)
-    out = (2.0 * exchange - direct).astype(jnp.bfloat16)
+    exchange = exchange.reshape(S, per_dev, vr, NC, NV, NC).transpose(0, 1, 2, 4, 3, 5).reshape(dsum.shape)
+    out = (2.0 * exchange - dsum).astype(jnp.bfloat16)
+    out = out.reshape(S, per_dev, vr, NV, NC, NC).transpose(0, 1, 2, 4, 3, 5).reshape(S, per_dev, vr * NC, NV * NC)
     return jnp.swapaxes(out, 0, 1)
 
 

time: 71 us -> 73.9 us (1.041)
  waiting for transfers between devices: 4.96 us -> 1.27 us
  matrix products: 9.3 us -> 11.4 us
  other arithmetic: 4.55 us -> 6.6 us
  local copies, waits for them, and re-layouts: 17 us -> 18.6 us
    all_to_all x1, waiting for transfers between devices: 4.95 us -> 1.27 us  [shards(): got = lax.all_to_all(terms, 'pair', 0, 0, tiled=True)]
    reshape x2 -> x1, local copies, waits for them, and re-layouts: 4.23 us -> 0.99 us  [shards(): out.reshape(S, per_dev, vr, NV, NC, NC).transpose(0, 1, 2, 4, 3, 5)]
    reduce_sum x0 -> x1, local copies, waits for them, and re-layouts: none -> 2.86 us  [shards(): dsum = jnp.sum(got.astype(jnp.float32), axis=0)]
    transpose x0 -> x1, other arithmetic: none -> 2.48 us  [shards(): out.reshape(S, per_dev, vr, NV, NC, NC).transpose(0, 1, 2, 4, 3, 5)]
    mul x0 -> x1, local copies, waits for them, and re-layouts: none -> 1.66 us  [shards(): out = (2.0 * exchange - dsum).astype(jnp.bfloat16)]
    dot_general x1, matrix products: 1.47 us -> 2.87 us  [shards(): jnp.einsum('abpg,bqg->abpq', weighted, own, preferred_element_type=jnp.fl...]
    transpose x1 -> x2, local copies, waits for them, and re-layouts: 2 us -> 0.94 us  [the longest x1 0.67 us: shards(): return jnp.swapaxes(out, 0, 1)]
    reshape x1, local copies, waits for them, and re-layouts: 0.83 us -> 1.88 us  [shards(): terms = terms.reshape(S, per_dev, npair, vr * NV, NC * NC)]
  transfers between devices with their start and end apart: 3 -> 3, of which waited for: 1 -> 1; matrix products, arithmetic and copies ran while one was open for 18% -> 23% of each run, Pallas kernels for 0% -> 0%
where the time goes in v8:
time: 73.9 us; the launch traced here: 73.1 us
  starting transfers between devices  32.5 us (44%)
  local copies, waits for them, and re-layouts  18.6 us (25%)
  matrix products  11.4 us (15%)
  other arithmetic  6.6 us (9%)
  between operations  2.68 us (4%)
  waiting for transfers between devices  1.27 us (2%)
    ppermute x2, starting transfers between devices, from_behind(): return lax.ppermute(value, axis, pairs)  27.2 us
    reshape x1, local copies, waits for them, and re-layouts, shards(): screen2d = screen.reshape(screen.shape[0] * ng, width)  7.81 us
    all_to_all x1, starting transfers between devices, shards(): got = lax.all_to_all(terms, 'pair', 0, 0, tiled=True)  5.33 us
    dot_general x2, matrix products, fields(): jnp.einsum('...pm,mg->...pg', prod, fit, preferred_element_type=jnp.float32)  3.75 us
    dot_general x1, matrix products, shards(): jnp.einsum('abpg,bqg->abpq', weighted, own, preferred_element_type=jnp.fl...  2.87 us
    reduce_sum x1, local copies, waits for them, and re-layouts, shards(): dsum = jnp.sum(got.astype(jnp.float32), axis=0)  2.86 us
    dot_general x1, matrix products, shards(): jnp.einsum('abpg,abqg->abpq', vale, screened, preferred_element_type=jnp....  2.64 us
    transpose x1, other arithmetic, shards(): out.reshape(S, per_dev, vr, NV, NC, NC).transpose(0, 1, 2, 4, 3, 5)  2.48 us
  transfers between devices with their start and end apart: 3, of which 1 were waited for; matrix products, arithmetic and copies ran while one was open for 23% of the time, Pallas kernels for 0%

profile of v8, /device:TPU:1, one launch (start us, length us, event | category | flops | bytes accessed | tf_op | source)
XLA Modules:
  0.0 73.1 jit_solution(9253878470963120029)
XLA Ops:
  0.0 24.8 %collective-permute-start = (bf16[2,32,512]{2,1,0:T(8,128)(2,1)}, bf16[2,32,512]{2,1,0:T(8,128)(2,1)S(1)}, u32[]{:S(2)}, u32[]{:S(2)}) collective-permute-start(bf16[2,32,512]{2,1,0:T(8,128)(2,1)} %param.5), channel_id=1, source_target_pairs={{0,1020},{4,0},{8,4},{12,8},{16,12},{20,16},{24,20},{28,24},{32,28... | collective-permute-start | bytes 196616 | tf_op jit(solution)/shard_map/ppermute | solution.py:14
  24.8 2.4 %collective-permute-start.1 = (bf16[2,32,512]{2,1,0:T(8,128)(2,1)}, bf16[2,32,512]{2,1,0:T(8,128)(2,1)S(1)}, u32[]{:S(2)}, u32[]{:S(2)}) collective-permute-start(bf16[2,32,512]{2,1,0:T(8,128)(2,1)} %param.5), channel_id=1, source_target_pairs={{0,1016},{4,1020},{8,0},{12,4},{16,8},{20,12},{24,16},{28,20},{32,... | collective-permute-start | bytes 196616 | tf_op jit(solution)/shard_map/ppermute | solution.py:14
  27.2 0.8 %slice_convert_fusion = (f32[2,16,512]{2,1,0:T(8,128)S(1)}, f32[2,16,512]{2,1,0:T(8,128)S(1)}) fusion(bf16[2,32,512]{2,1,0:T(8,128)(2,1)} %param.5), kind=kLoop, calls=%fused_computation.59 | loop fusion | flops 32768 | bytes 196608 | tf_op jit(solution)/shard_map/convert_element_type | solution.py:18
  28.0 1.4 %constant_dynamic-slice_fusion.1 = (s32[1,1]{0,1:T(1,128)}, s32[1,1]{0,1:T(1,128)}, s32[1,1]{0,1:T(1,128)}, s32[1,1]{0,1:T(1,128)}) fusion(s32[512,2]{0,1:T(2,128)} %param.9, s32[]{:T(128)S(6)} %select_n.28, s32[]{:T(128)S(6)} %select_n.30), kind=kLoop, calls=%fused_computation.68 | loop fusion | bytes 40 | tf_op jit(solution)/shard_map/dynamic_slice | solution.py:51
  32.0 7.8 %reshape.47 = bf16[5600,350]{0,1:T(8,128)(2,1)} reshape(bf16[4,1400,350]{1,0,2:T(4,128)(2,1)} %param.7) | data formatting | bytes 7840000 | tf_op jit(solution)/shard_map/reshape | solution.py:46
  39.8 0.1 fusion.24
  39.9 0.1 mul.131
  40.1 0.1 mul.147
  40.2 0.3 copy-done.2
  40.5 0.0 copy-done.4
  40.5 0.5 fusion.4
  41.1 1.7 %convolution_convert_fusion = bf16[2,2,256,1400]{2,3,1,0:T(8,128)(2,1)S(1)} fusion(bf16[2,2,256,512]{3,2,1,0:T(8,128)(2,1)S(1)} %get-tuple-element.13, bf16[512,1400]{0,1:T(8,128)(2,1)S(1)} %copy-done), kind=kOutput, calls=%fused_computation | convolution fusion | flops 1469440000 | bytes 5349376 | tf_op jit(solution)/shard_map/...pm,mg->...pg/dot_general | solution.py:25
  42.8 0.4 copy-done.1
  43.2 0.5 fusion.19
  43.8 0.5 fusion.20
  44.3 0.5 fusion.21
  44.8 0.5 fusion.22
  45.4 0.8 %maximum_bitcast_fusion.1 = bf16[1,2,256,350]{2,3,1,0:T(8,128)(2,1)} fusion(bf16[1,256,350]{1,2,0:T(8,128)(2,1)S(1)} %fusion.22, bf16[1,256,350]{1,2,0:T(8,128)(2,1)S(1)} %fusion.21), kind=kLoop, calls=%fused_computation.48 | loop fusion | flops 179200 | bytes 716800 | tf_op jit(solution)/shard_map/stack | solution.py:55
  46.2 2.6 %convolution_convert_fusion.4 = bf16[2,2,256,256]{3,2,1,0:T(8,128)(2,1)} fusion(bf16[2,2,256,512]{3,2,1,0:T(8,128)(2,1)S(1)} %get-tuple-element.14, bf16[1,2,256,350]{2,3,1,0:T(8,128)(2,1)} %maximum_bitcast_fusion.1, bf16[1,2,256,350]{2,3,1,0:T(8,128)(2,1)S(1)} %maximum_bitcast_fusion, bf16[512,1400]{0,1:T(8,128)(2,1)S(1)} %copy-done, s32[]{:T(128)S(6)} %select_n.27), kind=kOutput, calls=%fused_computation.17 | convolution fusion | flops 551481344 | bytes 2652164 | tf_op jit(solution)/shard_map/abpg,abqg->abpq/dot_general | solution.py:57
  48.8 1.9 %copy.29 = bf16[2,2,4,64,256]{4,3,1,0,2:T(8,128)(2,1)} copy(bf16[2,2,4,64,256]{4,3,2,1,0:T(8,128)(2,1)} %bitcast.105) | data formatting | bytes 1048576 | tf_op jit(solution)/shard_map/reshape | solution.py:58
  50.7 5.3 %all-to-all-start = ((bf16[4,2,2,64,256]{4,3,2,1,0:T(8,128)(2,1)}), bf16[4,2,2,64,256]{4,3,2,1,0:T(8,128)(2,1)}, u32[]{:S(2)}, u32[]{:S(2)}) async-start(bf16[4,2,2,64,256]{4,3,2,1,0:T(8,128)(2,1)} %bitcast.101), calls=%async_computation | async-start | bytes 1048576 | tf_op jit(solution)/shard_map/all_to_all | solution.py:60
  56.1 2.1 %fusion = bf16[2,256,1400,1]{1,2,3,0:T(8,128)(2,1)} fusion(bf16[2,256,512]{2,1,0:T(8,128)(2,1)S(1)} %fusion.24, bf16[512,1400]{0,1:T(8,128)(2,1)S(1)} %copy-done), kind=kOutput, calls=%fused_computation.2 | convolution fusion | flops 734720000 | bytes 3391488 | tf_op jit(solution)/shard_map/...pm,mg->...pg/dot_general | solution.py:25
  58.1 0.1 multiply_convert_fusion
  58.2 2.9 %fusion.16 = f32[2,2,64,256]{3,2,0,1:T(8,128)} fusion(bf16[2,256,1400,1]{1,2,3,0:T(8,128)(2,1)} %fusion, bf16[2,2,64,512]{3,2,0,1:T(8,128)(2,1)S(1)} %bitcast.106, bf16[512,1400]{0,1:T(8,128)(2,1)S(1)} %copy-done, f32[1400]{0:T(1024)S(1)} %copy-done.6), kind=kOutput, calls=%fused_computation.24 | convolution fusion | flops 552001536 | bytes 3397088 | tf_op jit(solution)/shard_map/abpg,bqg->abpq/dot_general | solution.py:66
  61.1 1.7 %mul.143 = f32[2,2,4,16,16,16]{5,4,3,2,0,1:T(8,128)S(1)} reshape(f32[2,2,64,256]{3,2,0,1:T(8,128)} %fusion.16) | data formatting | bytes 524288 | tf_op jit(solution)/shard_map/mul | solution.py:68
  62.8 1.3 %all-to-all-done = bf16[4,2,2,64,256]{4,3,2,1,0:T(8,128)(2,1)} async-done(((bf16[4,2,2,64,256]{4,3,2,1,0:T(8,128)(2,1)}), bf16[4,2,2,64,256]{4,3,2,1,0:T(8,128)(2,1)}, u32[]{:S(2)}, u32[]{:S(2)}) %all-to-all-start) | async-done | bytes 524320 | tf_op jit(solution)/shard_map/all_to_all | solution.py:60
  64.0 1.8 %convert_reduce_fusion = f32[2,2,64,256]{3,2,1,0:T(8,128)} fusion(bf16[4,2,2,64,256]{4,3,2,1,0:T(8,128)(2,1)} %all-to-all-done), kind=kLoop, calls=%fused_computation.32 | loop fusion | flops 458752 | bytes 786432 | tf_op jit(solution)/shard_map/reduce_sum | solution.py:61
  65.8 2.9 %reduce_sum.12 = f32[2,2,4,16,16,16]{5,4,3,2,1,0:T(8,128)} reshape(f32[2,2,64,256]{3,2,1,0:T(8,128)} %convert_reduce_fusion) | data formatting | bytes 524288 | tf_op jit(solution)/shard_map/reduce_sum | solution.py:61
  68.7 2.5 %fusion.23 = bf16[2,2,4,16,16,16]{5,3,4,2,1,0:T(8,128)(2,1)S(1)} fusion(f32[2,2,4,16,16,16]{5,4,3,2,1,0:T(8,128)} %reduce_sum.12, f32[2,2,4,16,16,16]{5,4,3,2,0,1:T(8,128)S(1)} %mul.143), kind=kLoop, calls=%fused_computation.29 | loop fusion | flops 131072 | bytes 655360 | tf_op jit(solution)/shard_map/transpose | solution.py:69
  71.2 0.3 copy.16
  71.5 1.0 %reshape.49 = bf16[2,2,64,256]{3,2,1,0:T(8,128)(2,1)S(1)} reshape(bf16[2,2,4,16,16,16]{5,4,3,2,1,0:T(8,128)(2,1)S(1)} %copy.16) | data formatting | bytes 262144 | tf_op jit(solution)/shard_map/reshape | solution.py:69
  72.4 0.7 copy.17
  (15 shorter events, 0.1 us)
Async XLA Ops:
  0.0 41.1 %copy-start = (bf16[512,1400]{0,1:T(8,128)(2,1)S(1)}, bf16[512,1400]{0,1:T(8,128)(2,1)}, u32[]{:S(2)}) copy-start(bf16[512,1400]{0,1:T(8,128)(2,1)} %param.6) | copy-start | bytes 4300804
  0.0 39.9 %collective-permute-start = (bf16[2,32,512]{2,1,0:T(8,128)(2,1)}, bf16[2,32,512]{2,1,0:T(8,128)(2,1)S(1)}, u32[]{:S(2)}, u32[]{:S(2)}) collective-permute-start(bf16[2,32,512]{2,1,0:T(8,128)(2,1)} %param.5), channel_id=1, source_target_pairs={{0,1020},{4,0},{8,4},{12,8},{16,12},{20,16},{24,20},{28,24},{32,28... | collective-permute-start | bytes 196616 | tf_op jit(solution)/shard_map/ppermute | solution.py:14
  24.8 15.1 %collective-permute-start.1 = (bf16[2,32,512]{2,1,0:T(8,128)(2,1)}, bf16[2,32,512]{2,1,0:T(8,128)(2,1)S(1)}, u32[]{:S(2)}, u32[]{:S(2)}) collective-permute-start(bf16[2,32,512]{2,1,0:T(8,128)(2,1)} %param.5), channel_id=1, source_target_pairs={{0,1016},{4,1020},{8,0},{12,4},{16,8},{20,12},{24,16},{28,20},{32,... | collective-permute-start | bytes 196616 | tf_op jit(solution)/shard_map/ppermute | solution.py:14
  39.9 0.6 copy-start.2
  39.9 0.6 copy-start.4
  41.1 2.1 %copy-start.1 = (bf16[5600,350]{0,1:T(8,128)(2,1)S(1)}, bf16[5600,350]{0,1:T(8,128)(2,1)}, u32[]{:S(2)}) copy-start(bf16[5600,350]{0,1:T(8,128)(2,1)} %reshape.47) | copy-start | bytes 11760004
  50.7 13.3 %all-to-all-start = ((bf16[4,2,2,64,256]{4,3,2,1,0:T(8,128)(2,1)}), bf16[4,2,2,64,256]{4,3,2,1,0:T(8,128)(2,1)}, u32[]{:S(2)}, u32[]{:S(2)}) async-start(bf16[4,2,2,64,256]{4,3,2,1,0:T(8,128)(2,1)} %bitcast.101), calls=%async_computation | async-start | bytes 1048576 | tf_op jit(solution)/shard_map/all_to_all | solution.py:60
  56.1 2.1 %copy-start.3 = (bf16[2,32,512]{2,1,0:T(8,128)(2,1)S(1)}, bf16[2,32,512]{2,1,0:T(8,128)(2,1)}, u32[]{:S(2)}) copy-start(bf16[2,32,512]{2,1,0:T(8,128)(2,1)} %copy-done.2) | copy-start | bytes 196612
  56.1 2.1 %copy-start.5 = (bf16[2,32,512]{2,1,0:T(8,128)(2,1)S(1)}, bf16[2,32,512]{2,1,0:T(8,128)(2,1)}, u32[]{:S(2)}) copy-start(bf16[2,32,512]{2,1,0:T(8,128)(2,1)} %copy-done.4) | copy-start | bytes 196612
  56.1 2.1 %copy-start.6 = (f32[1400]{0:T(1024)S(1)}, f32[1400]{0:T(1024)}, u32[]{:S(2)}) copy-start(f32[1400]{0:T(1024)} %param.8) | copy-start | bytes 16804

commit v9 on v1

--- a/solution.py
+++ b/solution.py
@@ -59,7 +59,7 @@
     terms = jnp.moveaxis(terms, 2, 0)
     got = lax.all_to_all(terms, "pair", 0, 0, tiled=True)
     dsum = jnp.sum(got.astype(jnp.float32), axis=0)
-    direct = dsum.reshape(S, per_dev, vr, NV, NC, NC).transpose(0, 1, 2, 4, 3, 5).reshape(S, per_dev, vr * NC, NV * NC)
+    direct = jnp.swapaxes(dsum.reshape(S * per_dev * vr, NV, NC, NC), 1, 2).reshape(S, per_dev, vr * NC, NV * NC)
 
     row_chosen = lax.dynamic_slice_in_dim(rows, pair_index * vr, vr, 2)
     rowf = fields(row_chosen, rows[:, :, NV:], fitting)

time: 71 us -> 71 us (level)
  no operation moved by 1% of the time
where the time goes in v9:
time: 71 us; the launch traced here: 70.4 us
  starting transfers between devices  31.9 us (45%)
  local copies, waits for them, and re-layouts  17 us (24%)
  matrix products  9.32 us (13%)
  waiting for transfers between devices  4.96 us (7%)
  other arithmetic  4.55 us (6%)
  between operations  2.72 us (4%)
    ppermute x2, starting transfers between devices, from_behind(): return lax.ppermute(value, axis, pairs)  27.2 us
    reshape x1, local copies, waits for them, and re-layouts, shards(): screen2d = screen.reshape(screen.shape[0] * ng, width)  7.8 us
    all_to_all x1, waiting for transfers between devices, shards(): got = lax.all_to_all(terms, 'pair', 0, 0, tiled=True)  4.95 us
    all_to_all x1, starting transfers between devices, shards(): got = lax.all_to_all(terms, 'pair', 0, 0, tiled=True)  4.67 us
    dot_general x2, matrix products, fields(): jnp.einsum('...pm,mg->...pg', prod, fit, preferred_element_type=jnp.float32)  3.75 us
    reshape x1, local copies, waits for them, and re-layouts, shards(): jnp.swapaxes(dsum.reshape(S * per_dev * vr, NV, NC, NC), 1, 2)  2.56 us
    dot_general x4, matrix products, shards(): jnp.dot(cond[s, lk], inter, preferred_element_type=jnp.float32)  2.16 us
    transpose x1, local copies, waits for them, and re-layouts, shards(): jnp.swapaxes(dsum.reshape(S * per_dev * vr, NV, NC, NC), 1, 2)  2 us
  transfers between devices with their start and end apart: 3, of which 1 were waited for; matrix products, arithmetic and copies ran while one was open for 18% of the time, Pallas kernels for 0%

profile of v9, /device:TPU:1, one launch (start us, length us, event | category | flops | bytes accessed | tf_op | source)
XLA Modules:
  0.0 70.4 jit_solution(1449707007917271835)
XLA Ops:
  0.0 0.0 copy-start
  0.0 24.8 %collective-permute-start = (bf16[2,32,512]{2,1,0:T(8,128)(2,1)}, bf16[2,32,512]{2,1,0:T(8,128)(2,1)S(1)}, u32[]{:S(2)}, u32[]{:S(2)}) collective-permute-start(bf16[2,32,512]{2,1,0:T(8,128)(2,1)} %param.5), channel_id=1, source_target_pairs={{0,1020},{4,0},{8,4},{12,8},{16,12},{20,16},{24,20},{28,24},{32,28... | collective-permute-start | bytes 196616 | tf_op jit(solution)/shard_map/ppermute | solution.py:14
  24.8 2.4 %collective-permute-start.1 = (bf16[2,32,512]{2,1,0:T(8,128)(2,1)}, bf16[2,32,512]{2,1,0:T(8,128)(2,1)S(1)}, u32[]{:S(2)}, u32[]{:S(2)}) collective-permute-start(bf16[2,32,512]{2,1,0:T(8,128)(2,1)} %param.5), channel_id=1, source_target_pairs={{0,1016},{4,1020},{8,0},{12,4},{16,8},{20,12},{24,16},{28,20},{32,... | collective-permute-start | bytes 196616 | tf_op jit(solution)/shard_map/ppermute | solution.py:14
  27.2 0.8 %slice_convert_fusion.1 = (f32[2,16,512]{2,1,0:T(8,128)S(1)}, f32[2,16,512]{2,1,0:T(8,128)S(1)}) fusion(bf16[2,32,512]{2,1,0:T(8,128)(2,1)} %param.5), kind=kLoop, calls=%fused_computation.60 | loop fusion | flops 32768 | bytes 196608 | tf_op jit(solution)/shard_map/convert_element_type | solution.py:18
  28.0 1.5 %constant_dynamic-slice_fusion.1 = (s32[1,1]{0,1:T(1,128)}, s32[1,1]{0,1:T(1,128)}, s32[1,1]{0,1:T(1,128)}, s32[1,1]{0,1:T(1,128)}) fusion(s32[512,2]{0,1:T(2,128)} %param.9, s32[]{:T(128)S(6)} %select_n.28, s32[]{:T(128)S(6)} %select_n.30), kind=kLoop, calls=%fused_computation.68 | loop fusion | bytes 40 | tf_op jit(solution)/shard_map/dynamic_slice | solution.py:51
  32.1 7.8 %reshape.44 = bf16[5600,350]{0,1:T(8,128)(2,1)} reshape(bf16[4,1400,350]{1,0,2:T(4,128)(2,1)} %param.7) | data formatting | bytes 7840000 | tf_op jit(solution)/shard_map/reshape | solution.py:46
  39.9 0.0 collective-permute-done
  39.9 0.0 collective-permute-done.1
  39.9 0.1 mul.124
  40.0 0.1 mul.138
  40.2 0.5 fusion.4
  40.7 0.0 copy-done
  40.7 1.7 %convolution_convert_fusion = bf16[2,2,256,1400]{2,3,1,0:T(8,128)(2,1)S(1)} fusion(bf16[2,2,256,512]{3,2,1,0:T(8,128)(2,1)S(1)} %get-tuple-element.13, bf16[512,1400]{0,1:T(8,128)(2,1)S(1)} %copy-done), kind=kOutput, calls=%fused_computation | convolution fusion | flops 1469440000 | bytes 5349376 | tf_op jit(solution)/shard_map/...pm,mg->...pg/dot_general | solution.py:25
  42.4 0.4 copy-done.1
  42.9 0.5 fusion.24
  43.4 0.5 fusion.25
  44.0 0.5 fusion.26
  44.5 0.5 fusion.27
  45.0 0.8 %maximum_bitcast_fusion = bf16[1,2,256,350]{2,3,1,0:T(8,128)(2,1)} fusion(bf16[1,256,350]{1,2,0:T(8,128)(2,1)S(1)} %fusion.25, bf16[1,256,350]{1,2,0:T(8,128)(2,1)S(1)} %fusion.24), kind=kLoop, calls=%fused_computation.47 | loop fusion | flops 179200 | bytes 716800 | tf_op jit(solution)/shard_map/stack | solution.py:55
  45.8 0.8 %maximum_bitcast_fusion.1 = bf16[1,2,256,350]{2,3,1,0:T(8,128)(2,1)} fusion(bf16[1,256,350]{1,2,0:T(8,128)(2,1)S(1)} %fusion.27, bf16[1,256,350]{1,2,0:T(8,128)(2,1)S(1)} %fusion.26), kind=kLoop, calls=%fused_computation.48 | loop fusion | flops 179200 | bytes 716800 | tf_op jit(solution)/shard_map/stack | solution.py:55
  46.6 1.9 %convolution_convert_fusion.4 = bf16[2,2,256,256]{3,2,1,0:T(8,128)(2,1)S(1)} fusion(bf16[2,2,256,512]{3,2,1,0:T(8,128)(2,1)S(1)} %get-tuple-element.14, bf16[1,2,256,350]{2,3,1,0:T(8,128)(2,1)} %maximum_bitcast_fusion.1, bf16[1,2,256,350]{2,3,1,0:T(8,128)(2,1)} %maximum_bitcast_fusion, bf16[512,1400]{0,1:T(8,128)(2,1)S(1)} %copy-done, s32[]{:T(128)S(6)} %select_n.27), kind=kOutput, calls=%fused_computation.15 | convolution fusion | flops 551481344 | bytes 2650116 | tf_op jit(solution)/shard_map/abpg,abqg->abpq/dot_general | solution.py:57
  48.5 0.8 %copy.25 = bf16[2,2,4,64,256]{4,3,1,0,2:T(8,128)(2,1)} copy(bf16[2,2,4,64,256]{4,3,2,1,0:T(8,128)(2,1)S(1)} %bitcast.107) | data formatting | bytes 1048576 | tf_op jit(solution)/shard_map/reshape | solution.py:58
  49.4 4.7 %all-to-all-start = ((bf16[4,2,2,64,256]{4,3,2,1,0:T(8,128)(2,1)}), bf16[4,2,2,64,256]{4,3,2,1,0:T(8,128)(2,1)S(1)}, u32[]{:S(2)}, u32[]{:S(2)}) async-start(bf16[4,2,2,64,256]{4,3,2,1,0:T(8,128)(2,1)} %bitcast.103), calls=%async_computation | async-start | bytes 1048576 | tf_op jit(solution)/shard_map/all_to_all | solution.py:60
  54.0 0.1 fusion.31
  54.1 2.1 %fusion = bf16[2,256,1400,1]{1,2,3,0:T(8,128)(2,1)} fusion(bf16[2,256,512]{2,1,0:T(8,128)(2,1)S(1)} %fusion.31, bf16[512,1400]{0,1:T(8,128)(2,1)S(1)} %copy-done), kind=kOutput, calls=%fused_computation.2 | convolution fusion | flops 734720000 | bytes 3391488 | tf_op jit(solution)/shard_map/...pm,mg->...pg/dot_general | solution.py:25
  56.2 0.8 %multiply_convert_fusion = bf16[2,2,4,16,512]{4,3,2,0,1:T(8,128)(2,1)} fusion(s32[]{:T(128)S(6)} %select_n.26, bf16[1,2,32,512]{3,2,1,0:T(8,128)(2,1)S(1)} %bitcast.112, bf16[1,2,32,512]{3,2,1,0:T(8,128)(2,1)S(1)} %bitcast.110, f32[2,2,16,512]{3,2,1,0:T(8,128)S(1)} %get-tuple-element.6), kind=kLoop, calls=%fused_computation.46 | loop fusion | flops 294912 | bytes 524292 | tf_op jit(solution)/shard_map/convert_element_type | solution.py:20
  56.9 5.0 %all-to-all-done = bf16[4,2,2,64,256]{4,3,2,1,0:T(8,128)(2,1)S(1)} async-done(((bf16[4,2,2,64,256]{4,3,2,1,0:T(8,128)(2,1)}), bf16[4,2,2,64,256]{4,3,2,1,0:T(8,128)(2,1)S(1)}, u32[]{:S(2)}, u32[]{:S(2)}) %all-to-all-start) | async-done | bytes 524320 | tf_op jit(solution)/shard_map/all_to_all | solution.py:60
  61.9 0.8 %convert_reduce_fusion = f32[2,2,64,256]{3,2,1,0:T(8,128)} fusion(bf16[4,2,2,64,256]{4,3,2,1,0:T(8,128)(2,1)S(1)} %all-to-all-done), kind=kLoop, calls=%fused_computation.32 | loop fusion | flops 458752 | bytes 786432 | tf_op jit(solution)/shard_map/reduce_sum | solution.py:61
  62.7 1.7 %reshape.46 = f32[16,16,16,16]{3,2,1,0:T(8,128)S(1)} reshape(f32[2,2,64,256]{3,2,1,0:T(8,128)} %convert_reduce_fusion) | data formatting | bytes 524288 | tf_op jit(solution)/shard_map/reshape | solution.py:62
  64.3 2.0 %copy.14 = f32[16,16,16,16]{3,2,1,0:T(8,128)} copy(f32[16,16,16,16]{3,1,2,0:T(8,128)S(1)} %bitcast.104) | data formatting | bytes 524288 | tf_op jit(solution)/shard_map/transpose | solution.py:62
  66.3 2.6 %reshape.47 = f32[2,2,64,256]{3,2,1,0:T(8,128)S(1)} reshape(f32[16,16,16,16]{3,2,1,0:T(8,128)} %copy.14) | data formatting | bytes 524288 | tf_op jit(solution)/shard_map/reshape | solution.py:62
  69.0 1.5 %fusion.28 = bf16[2,2,64,256]{3,2,1,0:T(8,128)(2,1)} fusion(bf16[2,256,1400,1]{1,2,3,0:T(8,128)(2,1)S(1)} %copy-done.4, bf16[2,2,64,512]{3,2,0,1:T(8,128)(2,1)S(1)} %bitcast.108, bf16[512,1400]{0,1:T(8,128)(2,1)S(1)} %copy-done, f32[1400]{0:T(1024)S(1)} %copy-done.3, f32[2,2,64,256]{3,2,1,0:T(8,128)S(1)} %reshape.47), kind=kOutput, calls=%fused_computation.29 | convolution fusion | flops 552132608 | bytes 3528160 | tf_op jit(solution)/shard_map/abpg,bqg->abpq/dot_general | solution.py:67
  (8 shorter events, 0.0 us)
Async XLA Ops:
  0.0 40.7 %copy-start = (bf16[512,1400]{0,1:T(8,128)(2,1)S(1)}, bf16[512,1400]{0,1:T(8,128)(2,1)}, u32[]{:S(2)}) copy-start(bf16[512,1400]{0,1:T(8,128)(2,1)} %param.6) | copy-start | bytes 4300804
  0.0 39.9 %collective-permute-start = (bf16[2,32,512]{2,1,0:T(8,128)(2,1)}, bf16[2,32,512]{2,1,0:T(8,128)(2,1)S(1)}, u32[]{:S(2)}, u32[]{:S(2)}) collective-permute-start(bf16[2,32,512]{2,1,0:T(8,128)(2,1)} %param.5), channel_id=1, source_target_pairs={{0,1020},{4,0},{8,4},{12,8},{16,12},{20,16},{24,20},{28,24},{32,28... | collective-permute-start | bytes 196616 | tf_op jit(solution)/shard_map/ppermute | solution.py:14
  24.8 15.1 %collective-permute-start.1 = (bf16[2,32,512]{2,1,0:T(8,128)(2,1)}, bf16[2,32,512]{2,1,0:T(8,128)(2,1)S(1)}, u32[]{:S(2)}, u32[]{:S(2)}) collective-permute-start(bf16[2,32,512]{2,1,0:T(8,128)(2,1)} %param.5), channel_id=1, source_target_pairs={{0,1016},{4,1020},{8,0},{12,4},{16,8},{20,12},{24,16},{28,20},{32,... | collective-permute-start | bytes 196616 | tf_op jit(solution)/shard_map/ppermute | solution.py:14
  40.7 2.1 %copy-start.1 = (bf16[5600,350]{0,1:T(8,128)(2,1)S(1)}, bf16[5600,350]{0,1:T(8,128)(2,1)}, u32[]{:S(2)}) copy-start(bf16[5600,350]{0,1:T(8,128)(2,1)} %reshape.44) | copy-start | bytes 11760004
  49.4 12.5 %all-to-all-start = ((bf16[4,2,2,64,256]{4,3,2,1,0:T(8,128)(2,1)}), bf16[4,2,2,64,256]{4,3,2,1,0:T(8,128)(2,1)S(1)}, u32[]{:S(2)}, u32[]{:S(2)}) async-start(bf16[4,2,2,64,256]{4,3,2,1,0:T(8,128)(2,1)} %bitcast.103), calls=%async_computation | async-start | bytes 1048576 | tf_op jit(solution)/shard_map/all_to_all | solution.py:60
  66.3 2.6 %copy-start.2 = (bf16[2,2,4,16,512]{4,3,2,0,1:T(8,128)(2,1)S(1)}, bf16[2,2,4,16,512]{4,3,2,0,1:T(8,128)(2,1)}, u32[]{:S(2)}) copy-start(bf16[2,2,4,16,512]{4,3,2,0,1:T(8,128)(2,1)} %multiply_convert_fusion) | copy-start | bytes 786436
  66.3 2.6 %copy-start.3 = (f32[1400]{0:T(1024)S(1)}, f32[1400]{0:T(1024)}, u32[]{:S(2)}) copy-start(f32[1400]{0:T(1024)} %param.8) | copy-start | bytes 16804
  66.3 2.6 %copy-start.4 = (bf16[2,256,1400,1]{1,2,3,0:T(8,128)(2,1)S(1)}, bf16[2,256,1400,1]{1,2,3,0:T(8,128)(2,1)}, u32[]{:S(2)}) copy-start(bf16[2,256,1400,1]{1,2,3,0:T(8,128)(2,1)} %fusion) | copy-start | bytes 4300804
